TPU v7x, 128 devices: a whole 4x4x4 slice. The times are simulated.
128 devices in a mesh: seq: 16 (over y, z), row: 2 (over core), col: 4 (over x).
Axes of the slice: x: 4, y: 4, z: 4, core: 2. Of those that a mesh axis runs over, the one named last changes fastest.
Arguments:
- hidden_in: bfloat16 [256, 1536], P('seq'), may hold values from -40 to 40
- attn_gain: float32 [1536], replicated, may hold values from 0.25 to 1.75
- w_query: bfloat16 [1536, 1536], P('seq', ('row', 'col')), may hold values from -0.15625 to 0.15625
- w_keyval: bfloat16 [1536, 1024], P('seq', ('row', 'col')), may hold values from -0.15625 to 0.15625
- w_out: bfloat16 [1536, 1536], P(('row', 'col'), 'seq'), may hold values from -0.15625 to 0.15625
- kv_cache: bfloat16 [64, 24576, 1024], P(None, 'seq', ('row', 'col')), may hold values from -360 to 360
- cache_len: int32 [64], replicated, may hold values from 1 to 24576, as said below
- ffn_gain: float32 [1536], replicated, may hold values from 0.25 to 1.75
- w_router: float32 [1536, 16], replicated, may hold values from -0.15625 to 0.15625
- routes: int32 [256, 2], replicated, may hold values from 0 to 15, all different within a row; in each aligned block of 256 rows (0 to 255, 256 to 511, ...) at most 64 rows name the same one
- w_gate_up: bfloat16 [16, 1536, 2, 1024], P('seq', 'row', None, 'col'), may hold values from -0.15625 to 0.15625
- w_down: bfloat16 [16, 1024, 1536], P('seq', 'col', 'row'), may hold values from -0.1875 to 0.1875
- final_gain: float32 [1536], replicated, may hold values from 0.25 to 1.75
- w_head: bfloat16 [1536, 65536], P('row', ('seq', 'col')), may hold values from -1.75 to 1.75
- targets: int32 [256], replicated, may hold values from 0 to 65535
Outputs:
- layer_out: bfloat16 [256, 1536], P(('seq', 'col'), 'row')
- logprob: float32 [256], replicated
Inputs may be any that keep to these rules, and one draw needn't show every extreme that they name: `cache_len`: lengths are uneven; some request has exactly 24576 cached positions. `routes`: the two experts of a row differ; each expert is named by at most 64 rows, a bound that some block reaches.
All inputs are finite; a program needn't handle non-finite values.
Results may differ from a plain program's by a relative error of at most 0.0044.
Values may be sent and summed in bfloat16 or wider, within the bound.
No kernel may reach another device: no remote copies, remote signals or barrier semaphores. Data moves between devices by JAX's collectives and lax.ppermute only.
A program may use at most 128 MiB of HBM per device.

v0:
```python
import jax
import jax.numpy as jnp
from jax import lax
from jax.sharding import PartitionSpec as P

HD = 64
EXP_DEV = 1
TOP = 2
NEW = 4


EPSILON = 1e-05
NEG_LARGE = -1e30


def combined_all(shard, axis, combine):
    everything = jax.tree.map(lambda part: lax.all_gather(part, axis), shard)
    initial = jax.tree.map(lambda part: part[0], everything)

    def lap(k, so_far):
        return combine(so_far, jax.tree.map(lambda part: part[k], everything))

    return lax.fori_loop(1, lax.axis_size(axis), lap, initial)


def radices_of(axes):
    names = (axes,) if isinstance(axes, str) else tuple(axes)
    radices = []
    for name in reversed(names):
        size = lax.axis_size(name)
        while size > 1:
            radix = 4 if size % 4 == 0 else 2
            radices.append(radix)
            size //= radix
    return radices


def group_exchange(value, axes, stride, radix, count, chunks=None):
    digit = (lax.axis_index(axes) // stride) % radix
    received = [value if chunks is None else chunks(digit)]
    for offset in range(1, radix):
        pairs = []
        for i in range(count):
            own = (i // stride) % radix
            pairs.append((i, i + ((own + offset) % radix - own) * stride))
        sent = value if chunks is None else chunks((digit + offset) % radix)
        received.append(lax.ppermute(sent, axes, pairs))
    ordered = []
    for source in range(radix):
        offset = (digit - source) % radix
        picked = received[0]
        for other in range(1, radix):
            picked = jnp.where(offset == other, received[other], picked)
        ordered.append(picked)
    return ordered


def fold(parts, combine):
    while len(parts) > 1:
        parts = [combine(parts[i], parts[i + 1]) for i in range(0, len(parts), 2)]
    return parts[0]


def packer(value):
    edges = [0]
    for part in value:
        edges.append(edges[-1] + part.shape[-1])

    def split(packed):
        return tuple(packed[..., edges[i] : edges[i + 1]] for i in range(len(value)))

    def combine_with(combine):
        return lambda a, b: jnp.concatenate(combine(split(a), split(b)), axis=-1)

    return jnp.concatenate(value, axis=-1), split, combine_with


def butterfly_merge(value, axes, count, combine):
    packed, split, combine_with = packer(value)
    stride = 1
    for radix in radices_of(axes):
        packed = fold(group_exchange(packed, axes, stride, radix, count), combine_with(combine))
        stride *= radix
    return split(packed)


def scatter_steps(packed, axes, count, joined):
    radices = radices_of(axes)
    strides = [1]
    for radix in radices:
        strides.append(strides[-1] * radix)
    for position in reversed(range(len(radices))):
        radix = radices[position]
        size = packed.shape[0] // radix
        whole = packed
        chunks = lambda k, whole=whole, size=size: lax.dynamic_slice_in_dim(whole, k * size, size, 0)
        parts = group_exchange(whole, axes, strides[position], radix, count, chunks)
        packed = fold(parts, joined)
    return packed


def halving_merge(value, axes, count, combine):
    packed, split, combine_with = packer(value)
    return split(scatter_steps(packed, axes, count, combine_with(combine)))


def butterfly_sum(value, axes, count):
    stride = 1
    for radix in radices_of(axes):
        value = fold(group_exchange(value, axes, stride, radix, count), lambda a, b: a + b)
        stride *= radix
    return value


def halving_scatter(value, axes, count):
    return scatter_steps(value, axes, count, lambda a, b: a + b)


def doubling_gather(value, axes, count):
    stride = 1
    for radix in radices_of(axes):
        value = jnp.concatenate(group_exchange(value, axes, stride, radix, count), axis=0)
        stride *= radix
    return value


def merge_logsumexp(first, second):
    high_a, sums_a, picked_a = first
    high_b, sums_b, picked_b = second
    highest = jnp.maximum(high_a, high_b)
    return (
        highest,
        sums_a * jnp.exp(high_a - highest) + sums_b * jnp.exp(high_b - highest),
        picked_a + picked_b,
    )


def rms_scale(values, gain):
    mean_square = jnp.mean(values * values, axis=-1, keepdims=True)
    return values * lax.rsqrt(mean_square + EPSILON) * gain


def final_scale(state, gain_half, width):
    squares = lax.psum(jnp.sum(state * state, axis=-1), "row")
    return (state * lax.rsqrt(squares[:, None] / width + EPSILON) * gain_half).astype(jnp.bfloat16)


def merge_softmax(first, second):
    high_a, sums_a, mixed_a = first
    high_b, sums_b, mixed_b = second
    highest = jnp.maximum(high_a, high_b)
    factor_a = jnp.exp(high_a - highest)
    factor_b = jnp.exp(high_b - highest)
    shaped_a = mixed_a.reshape(highest.shape + (-1,)) * factor_a[..., None]
    shaped_b = mixed_b.reshape(highest.shape + (-1,)) * factor_b[..., None]
    return (
        highest,
        sums_a * factor_a + sums_b * factor_b,
        (shaped_a + shaped_b).reshape(mixed_a.shape),
    )


def on_device(
    hidden_in,
    attn_gain,
    w_query,
    w_keyval,
    w_out,
    kv_cache,
    cache_len,
    ffn_gain,
    w_router,
    routes,
    w_gate_up,
    w_down,
    final_gain,
    w_head,
    targets,
):
    seq_count = lax.axis_size("seq")
    seq_index = lax.axis_index("seq")
    col_index = lax.axis_index("col")
    row_index = lax.axis_index("row")
    block_index = lax.axis_index(("seq", "col"))
    own_count = hidden_in.shape[0]
    block_start = seq_index * own_count
    pieces = [hidden_in.reshape(-1), w_query.reshape(-1), w_keyval.reshape(-1)]
    bounds = [0]
    for piece in pieces:
        bounds.append(bounds[-1] + piece.shape[0])
    packed = lax.all_gather(jnp.concatenate(pieces), "seq", axis=0, tiled=False)
    shards = packed.shape[0]
    every_row = packed[:, bounds[0] : bounds[1]].reshape((-1,) + hidden_in.shape[1:])
    w_query_all = packed[:, bounds[1] : bounds[2]].reshape((-1,) + w_query.shape[1:])
    w_keyval_all = packed[:, bounds[2] : bounds[3]].reshape((-1,) + w_keyval.shape[1:])
    w_out_all = (
        doubling_gather(w_out[None], "seq", lax.axis_size("seq"))
        .transpose(1, 0, 2)
        .reshape(w_out.shape[0], -1)
    )
    total_rows = every_row.shape[0]
    requests = total_rows // NEW
    width = every_row.shape[1]
    half = width // lax.axis_size("row")
    col_start = row_index * half
    state_in = every_row.astype(jnp.float32)
    normed_in = rms_scale(state_in, attn_gain).astype(jnp.bfloat16)
    query_cols = w_query.shape[1]
    group = query_cols // HD
    query = jnp.dot(
        normed_in,
        w_query_all,
        preferred_element_type=jnp.float32,
    )
    fresh_kv = jnp.dot(
        normed_in,
        w_keyval_all,
        preferred_element_type=jnp.float32,
    )
    fresh_kv = fresh_kv.astype(jnp.bfloat16).reshape(requests, NEW, 2, HD)
    queries = query.reshape(requests, NEW * group, HD)
    scale = HD ** (-0.5)
    length_dev = kv_cache.shape[1]
    cached = kv_cache.reshape(requests, length_dev, 2, HD)
    cached_keys = cached[:, :, 0].astype(jnp.float32)
    cached_values = cached[:, :, 1].astype(jnp.float32)
    old_scores = (
        jnp.einsum("rqd,rpd->rqp", queries, cached_keys, precision=lax.Precision.HIGHEST) * scale
    )
    positions = seq_index * length_dev + jnp.arange(length_dev, dtype=jnp.int32)
    old_mask = (positions[None, :] < cache_len[:, None])[:, None, :]
    fresh_keys = fresh_kv[:, :, 0].astype(jnp.float32)
    fresh_values = fresh_kv[:, :, 1].astype(jnp.float32)
    new_scores = (
        jnp.einsum("rqd,rud->rqu", queries, fresh_keys, precision=lax.Precision.HIGHEST) * scale
    )
    token_of = jnp.arange(NEW * group, dtype=jnp.int32) // group
    new_mask = (
        (token_of[:, None] >= jnp.arange(NEW, dtype=jnp.int32)[None, :]) & (seq_index == 0)
    )[None]
    old_scores = jnp.where(old_mask, old_scores, NEG_LARGE)
    new_scores = jnp.where(new_mask, new_scores, NEG_LARGE)
    highest = jnp.maximum(jnp.max(old_scores, axis=-1), jnp.max(new_scores, axis=-1))
    old_weights = jnp.where(old_mask, jnp.exp(old_scores - highest[..., None]), 0.0)
    new_weights = jnp.where(new_mask, jnp.exp(new_scores - highest[..., None]), 0.0)
    totals = old_weights.sum(-1) + new_weights.sum(-1)
    mixed = jnp.einsum("rqp,rpd->rqd", old_weights, cached_values, precision=lax.Precision.HIGHEST)
    mixed = mixed + jnp.einsum(
        "rqu,rud->rqd", new_weights, fresh_values, precision=lax.Precision.HIGHEST
    )
    highest, totals, mixed = halving_merge(
        (highest, totals, mixed.reshape(requests, -1)), "seq", seq_count, merge_softmax
    )
    own_requests = requests // seq_count
    attended = mixed.reshape(own_requests, NEW * group, HD) / totals[..., None]
    attn_mix = attended.reshape(own_count, query_cols).astype(jnp.bfloat16)
    partial_out = jnp.dot(
        attn_mix,
        w_out_all,
        preferred_element_type=jnp.float32,
    )
    own_mid = hidden_in.astype(jnp.float32) + butterfly_sum(
        partial_out, ("row", "col"), lax.axis_size("row") * lax.axis_size("col")
    )
    own_normed = rms_scale(own_mid, ffn_gain).astype(jnp.bfloat16)
    normed_mid = doubling_gather(own_normed, "seq", seq_count)
    router = jnp.dot(normed_mid.astype(jnp.float32), w_router, precision=lax.Precision.HIGHEST)
    chosen = jnp.take_along_axis(router, routes, axis=1)
    probs = jax.nn.sigmoid(chosen - chosen[:, ::-1])
    capacity = 2 * total_rows * TOP // (EXP_DEV * seq_count)
    row_ids = jnp.arange(total_rows, dtype=jnp.int32)
    slot_ids = jnp.arange(capacity, dtype=jnp.int32)
    expert = seq_index * EXP_DEV + 0
    member = routes == expert
    in_row = jnp.any(member, axis=1)
    weight_row = jnp.sum(jnp.where(member, probs, 0.0), axis=1)
    ordering = jnp.cumsum(in_row.astype(jnp.int32)) - 1
    filled = jnp.sum(in_row.astype(jnp.int32))
    source = (
        jnp.zeros((capacity,), jnp.int32)
        .at[jnp.where(in_row, ordering, capacity)]
        .set(row_ids, mode="drop")
    )
    source_list = [source]
    weight_list = [jnp.where(slot_ids < filled, weight_row[source], 0.0)]
    source_all = jnp.stack(source_list)
    weight_all = jnp.stack(weight_list)
    normed_half = lax.dynamic_slice_in_dim(normed_mid, col_start, half, 1)
    expert_rows = normed_half[source_all]
    gate_part = jnp.einsum(
        "ecd,edgf->ecgf", expert_rows, w_gate_up, preferred_element_type=jnp.float32
    )
    gate_both = butterfly_sum(gate_part, "row", lax.axis_size("row"))
    expert_hidden = (jax.nn.silu(gate_both[:, :, 0]) * gate_both[:, :, 1]).astype(jnp.bfloat16)
    expert_result = jnp.einsum(
        "ecf,efd->ecd", expert_hidden, w_down, preferred_element_type=jnp.float32
    )
    weighted = (expert_result * weight_all[..., None]).reshape(-1, half)
    term = jnp.zeros((total_rows, half), jnp.float32).at[source_all.reshape(-1)].add(weighted)
    block_count = seq_count * lax.axis_size("col")
    out_count = total_rows // block_count
    block_mid = lax.dynamic_slice_in_dim(
        lax.dynamic_slice_in_dim(own_mid, col_index * out_count, out_count, 0), col_start, half, 1
    )
    state_out = halving_scatter(term, ("seq", "col"), block_count) + block_mid
    layer_out = state_out.astype(jnp.bfloat16)
    gain_half = lax.dynamic_slice_in_dim(final_gain, col_start, half, 0)
    normed_block = final_scale(state_out, gain_half, width)
    normed_out = doubling_gather(normed_block, ("seq", "col"), block_count)
    vocab_dev = w_head.shape[1]
    row_count = total_rows // lax.axis_size("row")
    logits = halving_scatter(
        jnp.dot(normed_out, w_head, preferred_element_type=jnp.float32),
        "row",
        lax.axis_size("row"),
    )
    own_targets = lax.dynamic_slice_in_dim(targets, row_index * row_count, row_count, 0)
    vocab_start = block_index * vocab_dev
    matches = (
        own_targets[:, None] == (vocab_start + jnp.arange(vocab_dev, dtype=jnp.int32))[None, :]
    )
    picked_local = jnp.sum(jnp.where(matches, logits, 0.0), axis=1)
    local_high = jnp.max(logits, axis=1)
    local_total = jnp.sum(jnp.exp(logits - local_high[:, None]), axis=1)
    row_high, row_total, picked = butterfly_merge(
        (local_high[None], local_total[None], picked_local[None]),
        ("seq", "col"),
        seq_count * lax.axis_size("col"),
        merge_logsumexp,
    )
    row_high, row_total, picked = row_high[0], row_total[0], picked[0]
    logprob_part = picked - (row_high + jnp.log(row_total))
    logprob = lax.all_gather(logprob_part, "row", axis=0, tiled=True)
    return (layer_out, logprob)


def solution(mesh):
    return jax.shard_map(
        on_device,
        mesh=mesh,
        in_specs=(
            P("seq", None),
            P(),
            P("seq", ("row", "col")),
            P("seq", ("row", "col")),
            P(("row", "col"), "seq"),
            P(None, "seq", ("row", "col")),
            P(),
            P(),
            P(),
            P(),
            P("seq", "row", None, "col"),
            P("seq", "col", "row"),
            P(),
            P("row", ("seq", "col")),
            P(),
        ),
        out_specs=(P(("seq", "col"), "row"), P()),
        check_vma=False,
    )
```

profile of v0, /device:TPU:1, one launch (start us, length us, event | category | flops | bytes accessed | tf_op | source)
XLA Modules:
  0.0 263.4 jit_solution(2613435094671922478)
XLA Ops:
  7.2 1.0 reshape.359
  8.2 0.9 reshape.360
  9.1 1.4 pad_maximum_fusion.4
  10.6 4.6 %collective-permute-start.6 = (bf16[1,192,96]{2,1,0:T(8,128)(2,1)}, bf16[1,192,96]{2,1,0:T(8,128)(2,1)S(1)}, u32[]{:S(2)}, u32[]{:S(2)}) collective-permute-start(bf16[1,192,96]{2,1,0:T(8,128)(2,1)} %bitcast.71), channel_id=1, source_target_pairs={{0,24},{8,0},{16,8},{24,16},{32,56},{40,32},{48,40},{56,48},{64,88... | collective-permute-start | bytes 110600 | tf_op jit(solution)/shard_map/ppermute | solution.py:47
  18.3 1.7 collective-permute-done.7
  21.0 3.0 %collective-permute-start.10 = (bf16[4,192,96]{2,1,0:T(8,128)(2,1)S(1)}, bf16[4,192,96]{2,1,0:T(8,128)(2,1)S(1)}, u32[]{:S(2)}, u32[]{:S(2)}) collective-permute-start(bf16[4,192,96]{2,1,0:T(8,128)(2,1)S(1)} %pad_maximum_fusion.2), channel_id=1, source_target_pairs={{0,64},{8,72},{16,80},{24,88},{32,96},{40,104},{48,112},{56,120},{... | collective-permute-start | bytes 442376 | tf_op jit(solution)/shard_map/ppermute | solution.py:47
  24.4 2.4 collective-permute-start.9
  28.7 32.6 %copy.57 = bf16[64,1536,128]{1,2,0:T(8,128)(2,1)} copy(bf16[64,1536,128]{2,1,0:T(8,128)(2,1)} %param.20) | data formatting | bytes 50331648 | tf_op args[5]
  63.3 1.9 reshape.416
  65.3 1.3 convert_multiply_fusion.1
  68.3 2.8 %mul.459 = f32[256,1536]{1,0:T(8,128)} reshape(f32[16,24576]{1,0:T(8,128)} %convert_multiply_fusion.1) | data formatting | bytes 3145728 | tf_op jit(solution)/shard_map/mul | solution.py:139
  71.1 1.6 reduce_sum.81
  75.1 2.0 fusion.10
  77.1 1.5 convert_element_type.69
  78.6 2.9 %reshape.362 = bf16[1536,192]{1,0:T(8,128)(2,1)} reshape(bf16[16,18432]{1,0:T(8,128)(2,1)} %slice.292) | data formatting | bytes 1179648 | tf_op jit(solution)/shard_map/reshape | solution.py:194
  81.5 1.5 fusion.90
  83.1 1.2 reshape.365
  85.5 8.2 %fusion.2 = (f32[64,12]{1,0:T(8,128)S(1)}, f32[64,12,1536]{2,1,0:T(8,128)S(1)}) fusion(pred[64,1536]{1,0:T(8,128)(4,1)S(1)} %broadcast_compare_fusion, f32[64,12,64]{2,1,0:T(8,128)S(1)} %reshape.363, bf16[64,1536,2,64]{1,3,2,0:T(8,128)(2,1)} %bitcast.66), kind=kOutput, calls=%fused_computation.11 | convolution fusion | flops 909507840 | bytes 17599488 | tf_op jit(solution)/shard_map/rqd,rpd->rqp/dot_general | solution.py:228
  93.7 12.9 %fusion = f32[64,12,64]{2,1,0:T(8,128)S(1)} fusion(bf16[64,1536,2,64]{1,3,2,0:T(8,128)(2,1)} %bitcast.67, f32[64,12,1536]{2,1,0:T(8,128)S(1)} %get-tuple-element.99, f32[64,12]{1,0:T(8,128)S(1)} %max.52, pred[64,1536]{1,0:T(8,128)(4,1)S(1)} %broadcast_compare_fusion), kind=kOutput, calls=%fused_computation.6 | convolution fusion | flops 910688256 | bytes 17599488 | tf_op jit(solution)/shard_map/rqp,rpd->rqd/dot_general | solution.py:247
  106.7 3.1 %fusion.3 = f32[64,12]{1,0:T(8,128)} fusion(f32[64,12,1536]{2,1,0:T(8,128)S(1)} %get-tuple-element.99, f32[64,12]{1,0:T(8,128)S(1)} %max.52, pred[64,1536]{1,0:T(8,128)(4,1)S(1)} %broadcast_compare_fusion), kind=kLoop, calls=%fused_computation.12 | loop fusion | flops 5897472 | bytes 4823040 | tf_op jit(solution)/shard_map/reduce_sum | solution.py:246
  113.2 1.0 select_select_fusion.7
  114.7 1.6 collective-permute-done.1
  122.0 1.5 collective-permute-done.4
  124.9 2.5 collective-permute-start.12
  129.0 3.4 %collective-permute-done.13 = f32[16,1536]{1,0:T(8,128)S(1)} collective-permute-done((f32[16,1536]{1,0:T(8,128)S(1)}, f32[16,1536]{1,0:T(8,128)S(1)}, u32[]{:S(2)}, u32[]{:S(2)}) %collective-permute-start.13) | collective-permute-done | bytes 98336 | tf_op jit(solution)/shard_map/ppermute | solution.py:47
  132.5 1.0 collective-permute-done.14
  133.5 7.0 %collective-permute-start.15 = (f32[16,1536]{1,0:T(8,128)S(1)}, f32[16,1536]{1,0:T(8,128)S(1)}, u32[]{:S(2)}, u32[]{:S(2)}) collective-permute-start(f32[16,1536]{1,0:T(8,128)S(1)} %add_add_fusion.2), channel_id=1, source_target_pairs={{0,4},{1,5},{2,6},{3,7},{4,0},{5,1},{6,2},{7,3},{8,12},{9,13},{10,... | collective-permute-start | bytes 294920 | tf_op jit(solution)/shard_map/ppermute | solution.py:47
  140.5 1.4 scatter_custom_fusion
  142.2 1.4 collective-permute-start.16
  144.6 0.9 collective-permute-done.16
  145.5 2.5 collective-permute-done.17
  148.1 1.1 collective-permute-done.18
  149.3 1.2 collective-permute-start.19
  152.6 2.1 collective-permute-done.19
  154.6 2.5 collective-permute-done.20
  157.1 5.8 %collective-permute-done.21 = bf16[64,1536]{1,0:T(8,128)(2,1)S(1)} collective-permute-done((bf16[64,1536]{1,0:T(8,128)(2,1)S(1)}, bf16[64,1536]{1,0:T(8,128)(2,1)S(1)}, u32[]{:S(2)}, u32[]{:S(2)}) %collective-permute-start.21) | collective-permute-done | bytes 196640 | tf_op jit(solution)/shard_map/ppermute | solution.py:47
  164.0 1.4 convolution_bitcast_fusion
  166.8 4.5 %gather_fusion.2 = f32[512]{0:T(512)S(1)} fusion(f32[256,16]{0,1:T(8,128)S(1)} %fusion.92, s32[512]{0:T(512)S(1)} %reshape.394), kind=kCustom, calls=%fused_computation.2 | custom fusion | bytes 8192 | tf_op jit(solution)/shard_map/jit(take_along_axis)/gather | solution.py:268
  173.5 1.2 scatter_custom_fusion.1
  176.3 5.0 %collective-permute-done.23 = f32[64,768]{1,0:T(8,128)S(1)} collective-permute-done((f32[64,768]{1,0:T(8,128)S(1)}, f32[64,768]{1,0:T(8,128)S(1)}, u32[]{:S(2)}, u32[]{:S(2)}) %collective-permute-start.23) | collective-permute-done | bytes 196640 | tf_op jit(solution)/shard_map/ppermute | solution.py:47
  181.3 1.5 collective-permute-done.24
  182.8 5.0 %collective-permute-done.25 = f32[64,768]{1,0:T(8,128)} collective-permute-done((f32[64,768]{1,0:T(8,128)S(1)}, f32[64,768]{1,0:T(8,128)}, u32[]{:S(2)}, u32[]{:S(2)}) %collective-permute-start.25) | collective-permute-done | bytes 196640 | tf_op jit(solution)/shard_map/ppermute | solution.py:47
  187.8 1.0 add_add_fusion
  190.5 1.3 collective-permute-done.26
  191.8 1.9 collective-permute-done.27
  196.9 1.8 collective-permute-done.30
  199.5 5.5 %psum.7 = f32[4]{0:T(128)S(1)} all-reduce(f32[4]{0:T(128)S(1)} %get-tuple-element.10), channel_id=1, replica_groups=mesh['seq'=16,'row'=2,'col'=4] {'row'}, use_global_device_ids=true, to_apply=%region_14.15 | all-reduce | flops 4 | bytes 32 | tf_op jit(solution)/shard_map/psum | solution.py:144
  205.6 1.7 collective-permute-start.32
  208.1 3.2 %collective-permute-done.33 = bf16[4,768]{1,0:T(4,128)(2,1)S(1)} collective-permute-done((bf16[4,768]{1,0:T(4,128)(2,1)S(1)}, bf16[4,768]{1,0:T(4,128)(2,1)S(1)}, u32[]{:S(2)}, u32[]{:S(2)}) %collective-permute-start.33) | collective-permute-done | bytes 6176 | tf_op jit(solution)/shard_map/ppermute | solution.py:47
  211.7 1.8 collective-permute-start.35
  214.5 3.2 %collective-permute-done.36 = bf16[16,768]{1,0:T(8,128)(2,1)S(1)} collective-permute-done((bf16[16,768]{1,0:T(8,128)(2,1)S(1)}, bf16[16,768]{1,0:T(8,128)(2,1)S(1)}, u32[]{:S(2)}, u32[]{:S(2)}) %collective-permute-start.36) | collective-permute-done | bytes 24608 | tf_op jit(solution)/shard_map/ppermute | solution.py:47
  219.7 2.0 collective-permute-done.38
  221.7 2.1 collective-permute-done.39
  223.7 1.0 collective-permute-done.40
  226.3 5.2 %collective-permute-start.41 = (f32[128,1024]{1,0:T(8,128)}, f32[128,1024]{1,0:T(8,128)S(1)}, u32[]{:S(2)}, u32[]{:S(2)}) collective-permute-start(f32[128,1024]{1,0:T(8,128)} %constant_dynamic-slice_fusion), channel_id=1, source_target_pairs={{0,4},{4,0},{1,5},{5,1},{2,6},{6,2},{3,7},{7,3},{8,12},{12,8},{9,1... | collective-permute-start | bytes 1572872 | tf_op jit(solution)/shard_map/ppermute | solution.py:47
  231.6 1.7 collective-permute-done.41
  234.0 0.9 collective-permute-start.43
  235.0 0.9 collective-permute-start.44
  236.2 1.8 collective-permute-done.43
  238.0 1.1 collective-permute-done.44
  241.6 2.1 collective-permute-done.46
  244.2 1.2 collective-permute-start.48
  246.8 2.5 collective-permute-done.49
  249.7 6.1 %all-gather.1 = f32[1,256]{1,0:T(1,128)S(1)} all-gather(f32[1,128]{1,0:T(1,128)S(1)} %fusion.56), channel_id=3, replica_groups=mesh['seq'=16,'row'=2,'col'=4] {'row'}, dimensions={1}, use_global_device_ids=true | all-gather | bytes 1536 | tf_op jit(solution)/shard_map/all_gather | solution.py:333
  (241 shorter events, 54.1 us)
Async XLA Ops:
  7.2 217.7 %copy-start = (bf16[768,1024]{1,0:T(8,128)(2,1)S(1)}, bf16[768,1024]{1,0:T(8,128)(2,1)}, u32[]{:S(2)}) copy-start(bf16[768,1024]{1,0:T(8,128)(2,1)} %param.28) | copy-start | bytes 4718596
  7.2 56.2 %all-gather.4.cloned.1.call-start = ((), (), s32[]{:S(2)}) async-start(), calls=%async_computation | async-start | bytes 1880064 | tf_op jit(solution)/shard_map/all_gather | solution.py:191
  10.6 7.7 %collective-permute-start.6 = (bf16[1,192,96]{2,1,0:T(8,128)(2,1)}, bf16[1,192,96]{2,1,0:T(8,128)(2,1)S(1)}, u32[]{:S(2)}, u32[]{:S(2)}) collective-permute-start(bf16[1,192,96]{2,1,0:T(8,128)(2,1)} %bitcast.71), channel_id=1, source_target_pairs={{0,24},{8,0},{16,8},{24,16},{32,56},{40,32},{48,40},{56,48},{64,88... | collective-permute-start | bytes 110600 | tf_op jit(solution)/shard_map/ppermute | solution.py:47
  15.2 4.8 %collective-permute-start.7 = (bf16[1,192,96]{2,1,0:T(8,128)(2,1)}, bf16[1,192,96]{2,1,0:T(8,128)(2,1)S(1)}, u32[]{:S(2)}, u32[]{:S(2)}) collective-permute-start(bf16[1,192,96]{2,1,0:T(8,128)(2,1)} %bitcast.72), channel_id=1, source_target_pairs={{0,16},{8,24},{16,0},{24,8},{32,48},{40,56},{48,32},{56,40},{64,80... | collective-permute-start | bytes 110600 | tf_op jit(solution)/shard_map/ppermute | solution.py:47
  15.2 4.9 %collective-permute-start.8 = (bf16[1,192,96]{2,1,0:T(8,128)(2,1)}, bf16[1,192,96]{2,1,0:T(8,128)(2,1)S(1)}, u32[]{:S(2)}, u32[]{:S(2)}) collective-permute-start(bf16[1,192,96]{2,1,0:T(8,128)(2,1)} %bitcast.73), channel_id=1, source_target_pairs={{0,8},{8,16},{16,24},{24,0},{32,40},{40,48},{48,56},{56,32},{64,72... | collective-permute-start | bytes 110600 | tf_op jit(solution)/shard_map/ppermute | solution.py:47
  20.9 41.5 %copy-start.8 = (bf16[1,192,96]{2,1,0:T(8,128)(2,1)}, bf16[1,192,96]{2,1,0:T(8,128)(2,1)S(1)}, u32[]{:S(2)}) copy-start(bf16[1,192,96]{2,1,0:T(8,128)(2,1)S(1)} %get-tuple-element.60) | copy-start | bytes 110596
  20.9 41.5 %copy-start.10 = (bf16[1,192,96]{2,1,0:T(8,128)(2,1)}, bf16[1,192,96]{2,1,0:T(8,128)(2,1)S(1)}, u32[]{:S(2)}) copy-start(bf16[1,192,96]{2,1,0:T(8,128)(2,1)S(1)} %get-tuple-element.61) | copy-start | bytes 110596
  21.0 41.4 %collective-permute-start.10 = (bf16[4,192,96]{2,1,0:T(8,128)(2,1)S(1)}, bf16[4,192,96]{2,1,0:T(8,128)(2,1)S(1)}, u32[]{:S(2)}, u32[]{:S(2)}) collective-permute-start(bf16[4,192,96]{2,1,0:T(8,128)(2,1)S(1)} %pad_maximum_fusion.2), channel_id=1, source_target_pairs={{0,64},{8,72},{16,80},{24,88},{32,96},{40,104},{48,112},{56,120},{... | collective-permute-start | bytes 442376 | tf_op jit(solution)/shard_map/ppermute | solution.py:47
  24.0 38.4 %collective-permute-start.11 = (bf16[4,192,96]{2,1,0:T(8,128)(2,1)S(1)}, bf16[4,192,96]{2,1,0:T(8,128)(2,1)S(1)}, u32[]{:S(2)}, u32[]{:S(2)}) collective-permute-start(bf16[4,192,96]{2,1,0:T(8,128)(2,1)S(1)} %pad_maximum_fusion.2), channel_id=1, source_target_pairs={{0,32},{8,40},{16,48},{24,56},{32,64},{40,72},{48,80},{56,88},{64,... | collective-permute-start | bytes 442376 | tf_op jit(solution)/shard_map/ppermute | solution.py:47
  24.4 38.0 %collective-permute-start.9 = (bf16[4,192,96]{2,1,0:T(8,128)(2,1)S(1)}, bf16[4,192,96]{2,1,0:T(8,128)(2,1)S(1)}, u32[]{:S(2)}, u32[]{:S(2)}) collective-permute-start(bf16[4,192,96]{2,1,0:T(8,128)(2,1)S(1)} %pad_maximum_fusion.2), channel_id=1, source_target_pairs={{0,96},{8,104},{16,112},{24,120},{32,0},{40,8},{48,16},{56,24},{64... | collective-permute-start | bytes 442376 | tf_op jit(solution)/shard_map/ppermute | solution.py:47
  106.7 13.7 %copy-start.1 = (bf16[4,192,96]{2,1,0:T(8,128)(2,1)S(1)}, bf16[4,192,96]{2,1,0:T(8,128)(2,1)}, u32[]{:S(2)}) copy-start(bf16[4,192,96]{2,1,0:T(8,128)(2,1)} %get-tuple-element.38) | copy-start | bytes 442372
  106.7 13.7 %copy-start.2 = (bf16[4,192,96]{2,1,0:T(8,128)(2,1)S(1)}, bf16[4,192,96]{2,1,0:T(8,128)(2,1)}, u32[]{:S(2)}) copy-start(bf16[4,192,96]{2,1,0:T(8,128)(2,1)} %get-tuple-element.39) | copy-start | bytes 442372
  110.5 18.0 %copy-start.21 = (s32[2]{0:T(128)S(1)}, s32[2]{0:T(128)}, u32[]{:S(2)}) copy-start(s32[2]{0:T(128)} %slice_reduce_fusion) | copy-start | bytes 28
  110.5 29.9 %copy-start.20 = (pred[256]{0:T(512)(128)(4,1)S(1)}, pred[256]{0:T(512)(128)(4,1)}, u32[]{:S(2)}) copy-start(pred[256]{0:T(512)(128)(4,1)} %copy-done.19) | copy-start | bytes 772
  110.5 31.4 %copy-start.13 = (bf16[16,1536]{1,0:T(8,128)(2,1)S(1)}, bf16[16,1536]{1,0:T(8,128)(2,1)}, u32[]{:S(2)}) copy-start(bf16[16,1536]{1,0:T(8,128)(2,1)} %param.15) | copy-start | bytes 147460
  110.7 31.4 %copy-start.15 = (f32[1536]{0:T(1024)S(1)}, f32[1536]{0:T(1024)}, u32[]{:S(2)}) copy-start(f32[1536]{0:T(1024)} %param.22) | copy-start | bytes 18436
  111.6 3.1 %collective-permute-start = (f32[16,792]{1,0:T(8,128)S(1)}, f32[16,792]{1,0:T(8,128)S(1)}, u32[]{:S(2)}, u32[]{:S(2)}) collective-permute-start(f32[16,792]{1,0:T(8,128)S(1)} %get-tuple-element.50), channel_id=1, source_target_pairs={{0,96},{8,104},{16,112},{24,120},{32,0},{40,8},{48,16},{56,24},{64... | collective-permute-start | bytes 152072 | tf_op jit(solution)/shard_map/ppermute | solution.py:47
  111.7 4.6 %collective-permute-start.1 = (f32[16,792]{1,0:T(8,128)S(1)}, f32[16,792]{1,0:T(8,128)S(1)}, u32[]{:S(2)}, u32[]{:S(2)}) collective-permute-start(f32[16,792]{1,0:T(8,128)S(1)} %get-tuple-element.49), channel_id=1, source_target_pairs={{0,64},{8,72},{16,80},{24,88},{32,96},{40,104},{48,112},{56,120},{... | collective-permute-start | bytes 152072 | tf_op jit(solution)/shard_map/ppermute | solution.py:47
  112.6 4.5 %collective-permute-start.2 = (f32[16,792]{1,0:T(8,128)S(1)}, f32[16,792]{1,0:T(8,128)S(1)}, u32[]{:S(2)}, u32[]{:S(2)}) collective-permute-start(f32[16,792]{1,0:T(8,128)S(1)} %get-tuple-element.48), channel_id=1, source_target_pairs={{0,32},{8,40},{16,48},{24,56},{32,64},{40,72},{48,80},{56,88},{64,... | collective-permute-start | bytes 152072 | tf_op jit(solution)/shard_map/ppermute | solution.py:47
  118.7 3.4 %collective-permute-start.3 = (f32[4,792]{1,0:T(4,128)S(1)}, f32[4,792]{1,0:T(4,128)S(1)}, u32[]{:S(2)}, u32[]{:S(2)}) collective-permute-start(f32[4,792]{1,0:T(4,128)S(1)} %get-tuple-element.74), channel_id=1, source_target_pairs={{0,24},{8,0},{16,8},{24,16},{32,56},{40,32},{48,40},{56,48},{64,88... | collective-permute-start | bytes 38024 | tf_op jit(solution)/shard_map/ppermute | solution.py:47
  119.5 4.1 %collective-permute-start.4 = (f32[4,792]{1,0:T(4,128)S(1)}, f32[4,792]{1,0:T(4,128)S(1)}, u32[]{:S(2)}, u32[]{:S(2)}) collective-permute-start(f32[4,792]{1,0:T(4,128)S(1)} %get-tuple-element.73), channel_id=1, source_target_pairs={{0,16},{8,24},{16,0},{24,8},{32,48},{40,56},{48,32},{56,40},{64,80... | collective-permute-start | bytes 38024 | tf_op jit(solution)/shard_map/ppermute | solution.py:47
  119.6 4.1 %collective-permute-start.5 = (f32[4,792]{1,0:T(4,128)S(1)}, f32[4,792]{1,0:T(4,128)S(1)}, u32[]{:S(2)}, u32[]{:S(2)}) collective-permute-start(f32[4,792]{1,0:T(4,128)S(1)} %get-tuple-element.72), channel_id=1, source_target_pairs={{0,8},{8,16},{16,24},{24,0},{32,40},{40,48},{48,56},{56,32},{64,72... | collective-permute-start | bytes 38024 | tf_op jit(solution)/shard_map/ppermute | solution.py:47
  121.1 45.0 %copy-start.14 = (f32[1536,16]{0,1:T(8,128)S(1)}, f32[1536,16]{0,1:T(8,128)}, u32[]{:S(2)}) copy-start(f32[1536,16]{0,1:T(8,128)} %param.23) | copy-start | bytes 294916
  124.9 4.2 %collective-permute-start.12 = (f32[16,1536]{1,0:T(8,128)S(1)}, f32[16,1536]{1,0:T(8,128)S(1)}, u32[]{:S(2)}, u32[]{:S(2)}) collective-permute-start(f32[16,1536]{1,0:T(8,128)S(1)} %fusion.91), channel_id=1, source_target_pairs={{0,3},{1,0},{2,1},{3,2},{4,7},{5,4},{6,5},{7,6},{8,11},{9,8},{10,9... | collective-permute-start | bytes 294920 | tf_op jit(solution)/shard_map/ppermute | solution.py:47
  127.4 5.1 %collective-permute-start.13 = (f32[16,1536]{1,0:T(8,128)S(1)}, f32[16,1536]{1,0:T(8,128)S(1)}, u32[]{:S(2)}, u32[]{:S(2)}) collective-permute-start(f32[16,1536]{1,0:T(8,128)S(1)} %fusion.91), channel_id=1, source_target_pairs={{0,2},{1,3},{2,0},{3,1},{4,6},{5,7},{6,4},{7,5},{8,10},{9,11},{10,... | collective-permute-start | bytes 294920 | tf_op jit(solution)/shard_map/ppermute | solution.py:47
  127.9 5.5 %collective-permute-start.14 = (f32[16,1536]{1,0:T(8,128)S(1)}, f32[16,1536]{1,0:T(8,128)S(1)}, u32[]{:S(2)}, u32[]{:S(2)}) collective-permute-start(f32[16,1536]{1,0:T(8,128)S(1)} %fusion.91), channel_id=1, source_target_pairs={{0,1},{1,2},{2,3},{3,0},{4,5},{5,6},{6,7},{7,4},{8,9},{9,10},{10,1... | collective-permute-start | bytes 294920 | tf_op jit(solution)/shard_map/ppermute | solution.py:47
  133.5 8.4 %collective-permute-start.15 = (f32[16,1536]{1,0:T(8,128)S(1)}, f32[16,1536]{1,0:T(8,128)S(1)}, u32[]{:S(2)}, u32[]{:S(2)}) collective-permute-start(f32[16,1536]{1,0:T(8,128)S(1)} %add_add_fusion.2), channel_id=1, source_target_pairs={{0,4},{1,5},{2,6},{3,7},{4,0},{5,1},{6,2},{7,3},{8,12},{9,13},{10,... | collective-permute-start | bytes 294920 | tf_op jit(solution)/shard_map/ppermute | solution.py:47
  142.2 3.3 %collective-permute-start.16 = (bf16[16,1536]{1,0:T(8,128)(2,1)S(1)}, bf16[16,1536]{1,0:T(8,128)(2,1)S(1)}, u32[]{:S(2)}, u32[]{:S(2)}) collective-permute-start(bf16[16,1536]{1,0:T(8,128)(2,1)S(1)} %multiply_convert_fusion), channel_id=1, source_target_pairs={{0,24},{8,0},{16,8},{24,16},{32,56},{40,32},{48,40},{56,48},{64,88... | collective-permute-start | bytes 147464 | tf_op jit(solution)/shard_map/ppermute | solution.py:47
  143.6 4.5 %collective-permute-start.17 = (bf16[16,1536]{1,0:T(8,128)(2,1)S(1)}, bf16[16,1536]{1,0:T(8,128)(2,1)S(1)}, u32[]{:S(2)}, u32[]{:S(2)}) collective-permute-start(bf16[16,1536]{1,0:T(8,128)(2,1)S(1)} %multiply_convert_fusion), channel_id=1, source_target_pairs={{0,16},{8,24},{16,0},{24,8},{32,48},{40,56},{48,32},{56,40},{64,80... | collective-permute-start | bytes 147464 | tf_op jit(solution)/shard_map/ppermute | solution.py:47
  144.2 4.9 %collective-permute-start.18 = (bf16[16,1536]{1,0:T(8,128)(2,1)S(1)}, bf16[16,1536]{1,0:T(8,128)(2,1)S(1)}, u32[]{:S(2)}, u32[]{:S(2)}) collective-permute-start(bf16[16,1536]{1,0:T(8,128)(2,1)S(1)} %multiply_convert_fusion), channel_id=1, source_target_pairs={{0,8},{8,16},{16,24},{24,0},{32,40},{40,48},{48,56},{56,32},{64,72... | collective-permute-start | bytes 147464 | tf_op jit(solution)/shard_map/ppermute | solution.py:47
  149.3 5.3 %collective-permute-start.19 = (bf16[64,1536]{1,0:T(8,128)(2,1)S(1)}, bf16[64,1536]{1,0:T(8,128)(2,1)S(1)}, u32[]{:S(2)}, u32[]{:S(2)}) collective-permute-start(bf16[64,1536]{1,0:T(8,128)(2,1)S(1)} %pad_maximum_fusion.3), channel_id=1, source_target_pairs={{0,96},{8,104},{16,112},{24,120},{32,0},{40,8},{48,16},{56,24},{64... | collective-permute-start | bytes 589832 | tf_op jit(solution)/shard_map/ppermute | solution.py:47
  150.5 6.6 %collective-permute-start.20 = (bf16[64,1536]{1,0:T(8,128)(2,1)S(1)}, bf16[64,1536]{1,0:T(8,128)(2,1)S(1)}, u32[]{:S(2)}, u32[]{:S(2)}) collective-permute-start(bf16[64,1536]{1,0:T(8,128)(2,1)S(1)} %pad_maximum_fusion.3), channel_id=1, source_target_pairs={{0,64},{8,72},{16,80},{24,88},{32,96},{40,104},{48,112},{56,120},{... | collective-permute-start | bytes 589832 | tf_op jit(solution)/shard_map/ppermute | solution.py:47
  151.1 11.8 %collective-permute-start.21 = (bf16[64,1536]{1,0:T(8,128)(2,1)S(1)}, bf16[64,1536]{1,0:T(8,128)(2,1)S(1)}, u32[]{:S(2)}, u32[]{:S(2)}) collective-permute-start(bf16[64,1536]{1,0:T(8,128)(2,1)S(1)} %pad_maximum_fusion.3), channel_id=1, source_target_pairs={{0,32},{8,40},{16,48},{24,56},{32,64},{40,72},{48,80},{56,88},{64,... | collective-permute-start | bytes 589832 | tf_op jit(solution)/shard_map/ppermute | solution.py:47
  165.4 7.8 %collective-permute-start.22 = (f32[1,64,2,256]{3,1,2,0:T(8,128)S(1)}, f32[1,64,2,256]{3,1,2,0:T(8,128)S(1)}, u32[]{:S(2)}, u32[]{:S(2)}) collective-permute-start(f32[1,64,2,256]{3,1,2,0:T(8,128)S(1)} %convolution_bitcast_fusion), channel_id=1, source_target_pairs={{0,4},{4,0},{1,5},{5,1},{2,6},{6,2},{3,7},{7,3},{8,12},{12,8},{9,1... | collective-permute-start | bytes 393224 | tf_op jit(solution)/shard_map/ppermute | solution.py:47
  166.8 29.1 %copy-start.18 = (f32[1536]{0:T(1024)S(1)}, f32[1536]{0:T(1024)}, u32[]{:S(2)}) copy-start(f32[1536]{0:T(1024)} %param.27) | copy-start | bytes 18436
  171.4 60.1 %copy-start.22 = (s32[256]{0:T(256)S(1)}, s32[256]{0:T(256)}, u32[]{:S(2)}) copy-start(s32[256]{0:T(256)} %param.29) | copy-start | bytes 3076
  174.7 6.6 %collective-permute-start.23 = (f32[64,768]{1,0:T(8,128)S(1)}, f32[64,768]{1,0:T(8,128)S(1)}, u32[]{:S(2)}, u32[]{:S(2)}) collective-permute-start(f32[64,768]{1,0:T(8,128)S(1)} %get-tuple-element.31), channel_id=1, source_target_pairs={{0,96},{1,97},{2,98},{3,99},{8,104},{9,105},{10,106},{11,107},{16,... | collective-permute-start | bytes 589832 | tf_op jit(solution)/shard_map/ppermute | solution.py:47
  175.1 7.7 %collective-permute-start.24 = (f32[64,768]{1,0:T(8,128)S(1)}, f32[64,768]{1,0:T(8,128)S(1)}, u32[]{:S(2)}, u32[]{:S(2)}) collective-permute-start(f32[64,768]{1,0:T(8,128)S(1)} %get-tuple-element.30), channel_id=1, source_target_pairs={{0,64},{1,65},{2,66},{3,67},{8,72},{9,73},{10,74},{11,75},{16,80},... | collective-permute-start | bytes 589832 | tf_op jit(solution)/shard_map/ppermute | solution.py:47
  175.7 12.1 %collective-permute-start.25 = (f32[64,768]{1,0:T(8,128)S(1)}, f32[64,768]{1,0:T(8,128)}, u32[]{:S(2)}, u32[]{:S(2)}) collective-permute-start(f32[64,768]{1,0:T(8,128)S(1)} %get-tuple-element.29), channel_id=1, source_target_pairs={{0,32},{1,33},{2,34},{3,35},{8,40},{9,41},{10,42},{11,43},{16,48},... | collective-permute-start | bytes 589832 | tf_op jit(solution)/shard_map/ppermute | solution.py:47
  188.8 3.0 %collective-permute-start.26 = (f32[16,768]{1,0:T(8,128)S(1)}, f32[16,768]{1,0:T(8,128)S(1)}, u32[]{:S(2)}, u32[]{:S(2)}) collective-permute-start(f32[16,768]{1,0:T(8,128)S(1)} %get-tuple-element.53), channel_id=1, source_target_pairs={{0,24},{1,25},{2,26},{3,27},{8,0},{9,1},{10,2},{11,3},{16,8},{17,9... | collective-permute-start | bytes 147464 | tf_op jit(solution)/shard_map/ppermute | solution.py:47
  189.3 4.4 %collective-permute-start.27 = (f32[16,768]{1,0:T(8,128)S(1)}, f32[16,768]{1,0:T(8,128)S(1)}, u32[]{:S(2)}, u32[]{:S(2)}) collective-permute-start(f32[16,768]{1,0:T(8,128)S(1)} %get-tuple-element.52), channel_id=1, source_target_pairs={{0,16},{1,17},{2,18},{3,19},{8,24},{9,25},{10,26},{11,27},{16,0},{... | collective-permute-start | bytes 147464 | tf_op jit(solution)/shard_map/ppermute | solution.py:47
  189.8 4.5 %collective-permute-start.28 = (f32[16,768]{1,0:T(8,128)S(1)}, f32[16,768]{1,0:T(8,128)S(1)}, u32[]{:S(2)}, u32[]{:S(2)}) collective-permute-start(f32[16,768]{1,0:T(8,128)S(1)} %get-tuple-element.51), channel_id=1, source_target_pairs={{0,8},{1,9},{2,10},{3,11},{8,16},{9,17},{10,18},{11,19},{16,24},{1... | collective-permute-start | bytes 147464 | tf_op jit(solution)/shard_map/ppermute | solution.py:47
  194.3 2.6 collective-permute-start.29
  194.7 4.0 %collective-permute-start.30 = (f32[4,768]{1,0:T(4,128)S(1)}, f32[4,768]{1,0:T(4,128)S(1)}, u32[]{:S(2)}, u32[]{:S(2)}) collective-permute-start(f32[4,768]{1,0:T(4,128)S(1)} %get-tuple-element.76), channel_id=1, source_target_pairs={{0,2},{1,3},{2,0},{3,1},{8,10},{9,11},{10,8},{11,9},{16,18},{17,19... | collective-permute-start | bytes 36872 | tf_op jit(solution)/shard_map/ppermute | solution.py:47
  195.2 4.1 %collective-permute-start.31 = (f32[4,768]{1,0:T(4,128)S(1)}, f32[4,768]{1,0:T(4,128)S(1)}, u32[]{:S(2)}, u32[]{:S(2)}) collective-permute-start(f32[4,768]{1,0:T(4,128)S(1)} %get-tuple-element.75), channel_id=1, source_target_pairs={{0,1},{1,2},{2,3},{3,0},{8,9},{9,10},{10,11},{11,8},{16,17},{17,18... | collective-permute-start | bytes 36872 | tf_op jit(solution)/shard_map/ppermute | solution.py:47
  205.6 2.5 collective-permute-start.32
  207.3 4.0 %collective-permute-start.33 = (bf16[4,768]{1,0:T(4,128)(2,1)S(1)}, bf16[4,768]{1,0:T(4,128)(2,1)S(1)}, u32[]{:S(2)}, u32[]{:S(2)}) collective-permute-start(bf16[4,768]{1,0:T(4,128)(2,1)S(1)} %get-tuple-element.82), channel_id=1, source_target_pairs={{0,2},{1,3},{2,0},{3,1},{8,10},{9,11},{10,8},{11,9},{16,18},{17,19... | collective-permute-start | bytes 18440 | tf_op jit(solution)/shard_map/ppermute | solution.py:47
  208.0 3.7 %collective-permute-start.34 = (bf16[4,768]{1,0:T(4,128)(2,1)S(1)}, bf16[4,768]{1,0:T(4,128)(2,1)S(1)}, u32[]{:S(2)}, u32[]{:S(2)}) collective-permute-start(bf16[4,768]{1,0:T(4,128)(2,1)S(1)} %get-tuple-element.82), channel_id=1, source_target_pairs={{0,1},{1,2},{2,3},{3,0},{8,9},{9,10},{10,11},{11,8},{16,17},{17,18... | collective-permute-start | bytes 18440 | tf_op jit(solution)/shard_map/ppermute | solution.py:47
  211.7 2.7 %collective-permute-start.35 = (bf16[16,768]{1,0:T(8,128)(2,1)S(1)}, bf16[16,768]{1,0:T(8,128)(2,1)S(1)}, u32[]{:S(2)}, u32[]{:S(2)}) collective-permute-start(bf16[16,768]{1,0:T(8,128)(2,1)S(1)} %pad_maximum_fusion.7), channel_id=1, source_target_pairs={{0,24},{1,25},{2,26},{3,27},{8,0},{9,1},{10,2},{11,3},{16,8},{17,9... | collective-permute-start | bytes 73736 | tf_op jit(solution)/shard_map/ppermute | solution.py:47
  213.5 4.2 %collective-permute-start.36 = (bf16[16,768]{1,0:T(8,128)(2,1)S(1)}, bf16[16,768]{1,0:T(8,128)(2,1)S(1)}, u32[]{:S(2)}, u32[]{:S(2)}) collective-permute-start(bf16[16,768]{1,0:T(8,128)(2,1)S(1)} %pad_maximum_fusion.7), channel_id=1, source_target_pairs={{0,16},{1,17},{2,18},{3,19},{8,24},{9,25},{10,26},{11,27},{16,0},{... | collective-permute-start | bytes 73736 | tf_op jit(solution)/shard_map/ppermute | solution.py:47
  214.1 3.9 %collective-permute-start.37 = (bf16[16,768]{1,0:T(8,128)(2,1)S(1)}, bf16[16,768]{1,0:T(8,128)(2,1)S(1)}, u32[]{:S(2)}, u32[]{:S(2)}) collective-permute-start(bf16[16,768]{1,0:T(8,128)(2,1)S(1)} %pad_maximum_fusion.7), channel_id=1, source_target_pairs={{0,8},{1,9},{2,10},{3,11},{8,16},{9,17},{10,18},{11,19},{16,24},{1... | collective-permute-start | bytes 73736 | tf_op jit(solution)/shard_map/ppermute | solution.py:47
  218.1 3.5 %collective-permute-start.38 = (bf16[64,768]{1,0:T(8,128)(2,1)S(1)}, bf16[64,768]{1,0:T(8,128)(2,1)S(1)}, u32[]{:S(2)}, u32[]{:S(2)}) collective-permute-start(bf16[64,768]{1,0:T(8,128)(2,1)S(1)} %pad_maximum_fusion.5), channel_id=1, source_target_pairs={{0,96},{1,97},{2,98},{3,99},{8,104},{9,105},{10,106},{11,107},{16,... | collective-permute-start | bytes 294920 | tf_op jit(solution)/shard_map/ppermute | solution.py:47
  218.7 5.0 %collective-permute-start.39 = (bf16[64,768]{1,0:T(8,128)(2,1)S(1)}, bf16[64,768]{1,0:T(8,128)(2,1)S(1)}, u32[]{:S(2)}, u32[]{:S(2)}) collective-permute-start(bf16[64,768]{1,0:T(8,128)(2,1)S(1)} %pad_maximum_fusion.5), channel_id=1, source_target_pairs={{0,64},{1,65},{2,66},{3,67},{8,72},{9,73},{10,74},{11,75},{16,80},... | collective-permute-start | bytes 294920 | tf_op jit(solution)/shard_map/ppermute | solution.py:47
  219.1 5.6 %collective-permute-start.40 = (bf16[64,768]{1,0:T(8,128)(2,1)S(1)}, bf16[64,768]{1,0:T(8,128)(2,1)S(1)}, u32[]{:S(2)}, u32[]{:S(2)}) collective-permute-start(bf16[64,768]{1,0:T(8,128)(2,1)S(1)} %pad_maximum_fusion.5), channel_id=1, source_target_pairs={{0,32},{1,33},{2,34},{3,35},{8,40},{9,41},{10,42},{11,43},{16,48},... | collective-permute-start | bytes 294920 | tf_op jit(solution)/shard_map/ppermute | solution.py:47
  226.3 6.9 %collective-permute-start.41 = (f32[128,1024]{1,0:T(8,128)}, f32[128,1024]{1,0:T(8,128)S(1)}, u32[]{:S(2)}, u32[]{:S(2)}) collective-permute-start(f32[128,1024]{1,0:T(8,128)} %constant_dynamic-slice_fusion), channel_id=1, source_target_pairs={{0,4},{4,0},{1,5},{5,1},{2,6},{6,2},{3,7},{7,3},{8,12},{12,8},{9,1... | collective-permute-start | bytes 1572872 | tf_op jit(solution)/shard_map/ppermute | solution.py:47
  233.7 2.5 collective-permute-start.42
  234.0 3.9 %collective-permute-start.43 = (f32[1,384]{1,0:T(1,128)S(1)}, f32[1,384]{1,0:T(1,128)S(1)}, u32[]{:S(2)}, u32[]{:S(2)}) collective-permute-start(f32[1,384]{1,0:T(1,128)S(1)} %pad_maximum_fusion.8), channel_id=1, source_target_pairs={{0,2},{1,3},{2,0},{3,1},{8,10},{9,11},{10,8},{11,9},{16,18},{17,19... | collective-permute-start | bytes 4616 | tf_op jit(solution)/shard_map/ppermute | solution.py:47
  235.0 4.1 %collective-permute-start.44 = (f32[1,384]{1,0:T(1,128)S(1)}, f32[1,384]{1,0:T(1,128)S(1)}, u32[]{:S(2)}, u32[]{:S(2)}) collective-permute-start(f32[1,384]{1,0:T(1,128)S(1)} %pad_maximum_fusion.8), channel_id=1, source_target_pairs={{0,1},{1,2},{2,3},{3,0},{8,9},{9,10},{10,11},{11,8},{16,17},{17,18... | collective-permute-start | bytes 4616 | tf_op jit(solution)/shard_map/ppermute | solution.py:47
  239.1 2.5 collective-permute-start.45
  239.8 3.9 %collective-permute-start.46 = (f32[1,384]{1,0:T(1,128)S(1)}, f32[1,384]{1,0:T(1,128)S(1)}, u32[]{:S(2)}, u32[]{:S(2)}) collective-permute-start(f32[1,384]{1,0:T(1,128)S(1)} %pad_maximum_fusion.9), channel_id=1, source_target_pairs={{0,16},{1,17},{2,18},{3,19},{8,24},{9,25},{10,26},{11,27},{16,0},{... | collective-permute-start | bytes 4616 | tf_op jit(solution)/shard_map/ppermute | solution.py:47
  240.5 3.6 %collective-permute-start.47 = (f32[1,384]{1,0:T(1,128)S(1)}, f32[1,384]{1,0:T(1,128)S(1)}, u32[]{:S(2)}, u32[]{:S(2)}) collective-permute-start(f32[1,384]{1,0:T(1,128)S(1)} %pad_maximum_fusion.9), channel_id=1, source_target_pairs={{0,8},{1,9},{2,10},{3,11},{8,16},{9,17},{10,18},{11,19},{16,24},{1... | collective-permute-start | bytes 4616 | tf_op jit(solution)/shard_map/ppermute | solution.py:47
  244.2 2.6 collective-permute-start.48
  245.4 3.9 %collective-permute-start.49 = (f32[1,384]{1,0:T(1,128)S(1)}, f32[1,384]{1,0:T(1,128)S(1)}, u32[]{:S(2)}, u32[]{:S(2)}) collective-permute-start(f32[1,384]{1,0:T(1,128)S(1)} %pad_maximum_fusion.10), channel_id=1, source_target_pairs={{0,64},{1,65},{2,66},{3,67},{8,72},{9,73},{10,74},{11,75},{16,80},... | collective-permute-start | bytes 4616 | tf_op jit(solution)/shard_map/ppermute | solution.py:47
  246.0 3.6 %collective-permute-start.50 = (f32[1,384]{1,0:T(1,128)S(1)}, f32[1,384]{1,0:T(1,128)S(1)}, u32[]{:S(2)}, u32[]{:S(2)}) collective-permute-start(f32[1,384]{1,0:T(1,128)S(1)} %pad_maximum_fusion.10), channel_id=1, source_target_pairs={{0,32},{1,33},{2,34},{3,35},{8,40},{9,41},{10,42},{11,43},{16,48},... | collective-permute-start | bytes 4616 | tf_op jit(solution)/shard_map/ppermute | solution.py:47
  (11 other events, 51.6 us)
Sparse Core Ops, SparseCore 0:
  10.7 47.0 all-gather.3
where the time goes:
time: 268 us; the launch traced here: 263 us
  waiting for transfers between devices  68.6 us (26%)
  local copies, waits for them, and re-layouts  64 us (24%)
  starting transfers between devices  53.1 us (20%)
  matrix products  27.2 us (10%)
  other arithmetic  23.6 us (9%)
  between operations  15.3 us (6%)
  blocking collectives  11.6 us (4%)
    ppermute x51, waiting for transfers between devices, group_exchange(): received.append(lax.ppermute(sent, axes, pairs))  68.5 us
    ppermute x51, starting transfers between devices, group_exchange(): received.append(lax.ppermute(sent, axes, pairs))  53.1 us
    unnamed x49, local copies, waits for them, and re-layouts  34.2 us
    dot_general x1, matrix products, on_device(): jnp.einsum('rqp,rpd->rqd', old_weights, cached_values, precision=lax.Prec...  12.9 us
    dot_general x1, matrix products, on_device(): jnp.einsum('rqd,rpd->rqp', queries, cached_keys, precision=lax.Precision....  8.24 us
    all_gather x1, blocking collectives, on_device(): logprob = lax.all_gather(logprob_part, 'row', axis=0, tiled=True)  6.11 us
    psum x1, blocking collectives, final_scale(): squares = lax.psum(jnp.sum(state * state, axis=-1), 'row')  5.46 us
  transfers between devices with their start and end apart: 52, of which 44 were waited for; matrix products, arithmetic and copies ran while one was open for 20% of the time, Pallas kernels for 0%

commit v1 on v0

--- a/solution.py
+++ b/solution.py
@@ -184,15 +184,14 @@
     block_index = lax.axis_index(("seq", "col"))
     own_count = hidden_in.shape[0]
     block_start = seq_index * own_count
-    pieces = [hidden_in.reshape(-1), w_query.reshape(-1), w_keyval.reshape(-1)]
+    pieces = [hidden_in.reshape(-1), jnp.concatenate([w_query, w_keyval], axis=1).reshape(-1)]
     bounds = [0]
     for piece in pieces:
         bounds.append(bounds[-1] + piece.shape[0])
     packed = lax.all_gather(jnp.concatenate(pieces), "seq", axis=0, tiled=False)
     shards = packed.shape[0]
     every_row = packed[:, bounds[0] : bounds[1]].reshape((-1,) + hidden_in.shape[1:])
-    w_query_all = packed[:, bounds[1] : bounds[2]].reshape((-1,) + w_query.shape[1:])
-    w_keyval_all = packed[:, bounds[2] : bounds[3]].reshape((-1,) + w_keyval.shape[1:])
+    w_both_all = packed[:, bounds[1] : bounds[2]].reshape(-1, w_query.shape[1] + w_keyval.shape[1])
     w_out_all = (
         doubling_gather(w_out[None], "seq", lax.axis_size("seq"))
         .transpose(1, 0, 2)
@@ -207,16 +206,9 @@
     normed_in = rms_scale(state_in, attn_gain).astype(jnp.bfloat16)
     query_cols = w_query.shape[1]
     group = query_cols // HD
-    query = jnp.dot(
-        normed_in,
-        w_query_all,
-        preferred_element_type=jnp.float32,
-    )
-    fresh_kv = jnp.dot(
-        normed_in,
-        w_keyval_all,
-        preferred_element_type=jnp.float32,
-    )
+    both = jnp.dot(normed_in, w_both_all, preferred_element_type=jnp.float32)
+    query = both[:, : w_query.shape[1]]
+    fresh_kv = both[:, w_query.shape[1] :]
     fresh_kv = fresh_kv.astype(jnp.bfloat16).reshape(requests, NEW, 2, HD)
     queries = query.reshape(requests, NEW * group, HD)
     scale = HD ** (-0.5)

time: 268 us -> 263 us (0.981)
  local copies, waits for them, and re-layouts: 64 us -> 59.9 us
    reshape x4 -> x3, local copies, waits for them, and re-layouts: 5.96 us -> 3.48 us  [the longest x1 2.46 us: on_device(): packed[:, bounds[1]:bounds[2]]]
    unnamed x49 -> x61, local copies, waits for them, and re-layouts: 34.2 us -> 34.2 us
  transfers between devices with their start and end apart: 52 -> 52, of which waited for: 44 -> 43; matrix products, arithmetic and copies ran while one was open for 20% -> 18% of each run, Pallas kernels for 0% -> 0%
where the time goes in v1:
time: 263 us; the launch traced here: 259 us
  waiting for transfers between devices  67.7 us (26%)
  local copies, waits for them, and re-layouts  59.9 us (23%)
  starting transfers between devices  53.3 us (20%)
  matrix products  25.9 us (10%)
  other arithmetic  24.8 us (9%)
  between operations  15.4 us (6%)
  blocking collectives  11.6 us (4%)
    ppermute x51, waiting for transfers between devices, group_exchange(): received.append(lax.ppermute(sent, axes, pairs))  67.6 us
    ppermute x51, starting transfers between devices, group_exchange(): received.append(lax.ppermute(sent, axes, pairs))  53.3 us
    unnamed x61, local copies, waits for them, and re-layouts  34.2 us
    dot_general x1, matrix products, on_device(): jnp.einsum('rqp,rpd->rqd', old_weights, cached_values, precision=lax.Prec...  12.9 us
    dot_general x1, matrix products, on_device(): jnp.einsum('rqd,rpd->rqp', queries, cached_keys, precision=lax.Precision....  8.29 us
    all_gather x1, blocking collectives, on_device(): logprob = lax.all_gather(logprob_part, 'row', axis=0, tiled=True)  6.11 us
    gather x5, local copies, waits for them, and re-layouts, on_device(): chosen = jnp.take_along_axis(router, routes, axis=1)  5.71 us
    psum x1, blocking collectives, final_scale(): squares = lax.psum(jnp.sum(state * state, axis=-1), 'row')  5.47 us
  transfers between devices with their start and end apart: 52, of which 43 were waited for; matrix products, arithmetic and copies ran while one was open for 18% of the time, Pallas kernels for 0%

profile of v1, /device:TPU:1, one launch (start us, length us, event | category | flops | bytes accessed | tf_op | source)
XLA Modules:
  0.0 258.6 jit_solution(3241095444712148656)
XLA Ops:
  7.2 1.0 pad_maximum_fusion.6
  9.9 4.6 %collective-permute-start.6 = (bf16[1,192,96]{2,1,0:T(8,128)(2,1)}, bf16[1,192,96]{2,1,0:T(8,128)(2,1)S(1)}, u32[]{:S(2)}, u32[]{:S(2)}) collective-permute-start(bf16[1,192,96]{2,1,0:T(8,128)(2,1)} %bitcast.68), channel_id=1, source_target_pairs={{0,24},{8,0},{16,8},{24,16},{32,56},{40,32},{48,40},{56,48},{64,88... | collective-permute-start | bytes 110600 | tf_op jit(solution)/shard_map/ppermute | solution.py:47
  16.0 1.3 bitcast_or_fusion
  17.3 1.4 broadcast_compare_fusion
  20.4 2.8 %collective-permute-start.9 = (bf16[4,192,96]{2,1,0:T(8,128)(2,1)S(1)}, bf16[4,192,96]{2,1,0:T(8,128)(2,1)S(1)}, u32[]{:S(2)}, u32[]{:S(2)}) collective-permute-start(bf16[4,192,96]{2,1,0:T(8,128)(2,1)S(1)} %pad_maximum_fusion.2), channel_id=1, source_target_pairs={{0,96},{8,104},{16,112},{24,120},{32,0},{40,8},{48,16},{56,24},{64... | collective-permute-start | bytes 442376 | tf_op jit(solution)/shard_map/ppermute | solution.py:47
  24.4 32.6 %copy.59 = bf16[64,1536,128]{1,2,0:T(8,128)(2,1)} copy(bf16[64,1536,128]{2,1,0:T(8,128)(2,1)} %param.20) | data formatting | bytes 50331648 | tf_op args[5]
  59.1 1.9 reshape.403
  61.1 1.3 convert_multiply_fusion.1
  62.4 1.1 slice.297
  63.4 2.8 %mul.457 = f32[256,1536]{1,0:T(8,128)} reshape(f32[16,24576]{1,0:T(8,128)} %convert_multiply_fusion.1) | data formatting | bytes 3145728 | tf_op jit(solution)/shard_map/mul | solution.py:139
  66.3 1.6 reduce_sum.81
  69.0 1.1 fusion.10
  70.1 1.5 convert_element_type.65
  71.6 2.5 reshape.350
  75.3 8.3 %fusion.2 = (f32[64,12]{1,0:T(8,128)S(1)}, f32[64,12,1536]{2,1,0:T(8,128)S(1)}) fusion(pred[64,1536]{1,0:T(8,128)(4,1)} %broadcast_compare_fusion, f32[64,12,64]{2,1,0:T(8,128)S(1)} %reshape.351, bf16[64,1536,2,64]{1,3,2,0:T(8,128)(2,1)} %bitcast.63), kind=kOutput, calls=%fused_computation.11 | convolution fusion | flops 909507840 | bytes 17599488 | tf_op jit(solution)/shard_map/rqd,rpd->rqp/dot_general | solution.py:220
  84.2 12.9 %fusion = f32[64,12,64]{2,1,0:T(8,128)S(1)} fusion(bf16[64,1536,2,64]{1,3,2,0:T(8,128)(2,1)} %bitcast.64, f32[64,12,1536]{2,1,0:T(8,128)S(1)} %get-tuple-element.99, f32[64,12]{1,0:T(8,128)S(1)} %max.52, pred[64,1536]{1,0:T(8,128)(4,1)S(1)} %copy-done.1), kind=kOutput, calls=%fused_computation.6 | convolution fusion | flops 910688256 | bytes 17599488 | tf_op jit(solution)/shard_map/rqp,rpd->rqd/dot_general | solution.py:239
  97.2 3.0 %fusion.3 = f32[64,12]{1,0:T(8,128)} fusion(f32[64,12,1536]{2,1,0:T(8,128)S(1)} %get-tuple-element.99, f32[64,12]{1,0:T(8,128)S(1)} %max.52, pred[64,1536]{1,0:T(8,128)(4,1)S(1)} %copy-done.1), kind=kLoop, calls=%fused_computation.12 | loop fusion | flops 5897472 | bytes 4823040 | tf_op jit(solution)/shard_map/reduce_sum | solution.py:238
  102.7 2.1 collective-permute-start
  106.1 3.3 %collective-permute-done.1 = f32[16,792]{1,0:T(8,128)S(1)} collective-permute-done((f32[16,792]{1,0:T(8,128)S(1)}, f32[16,792]{1,0:T(8,128)S(1)}, u32[]{:S(2)}, u32[]{:S(2)}) %collective-permute-start.1) | collective-permute-done | bytes 50720 | tf_op jit(solution)/shard_map/ppermute | solution.py:47
  111.5 1.9 collective-permute-start.3
  113.4 1.2 collective-permute-start.4
  116.3 1.2 collective-permute-done.4
  117.5 0.9 collective-permute-done.5
  119.6 2.5 collective-permute-start.12
  123.9 3.2 %collective-permute-done.13 = f32[16,1536]{1,0:T(8,128)S(1)} collective-permute-done((f32[16,1536]{1,0:T(8,128)S(1)}, f32[16,1536]{1,0:T(8,128)S(1)}, u32[]{:S(2)}, u32[]{:S(2)}) %collective-permute-start.13) | collective-permute-done | bytes 98336 | tf_op jit(solution)/shard_map/ppermute | solution.py:47
  127.1 1.0 collective-permute-done.14
  128.1 7.0 %collective-permute-start.15 = (f32[16,1536]{1,0:T(8,128)S(1)}, f32[16,1536]{1,0:T(8,128)S(1)}, u32[]{:S(2)}, u32[]{:S(2)}) collective-permute-start(f32[16,1536]{1,0:T(8,128)S(1)} %add_add_fusion.2), channel_id=1, source_target_pairs={{0,4},{1,5},{2,6},{3,7},{4,0},{5,1},{6,2},{7,3},{8,12},{9,13},{10,... | collective-permute-start | bytes 294920 | tf_op jit(solution)/shard_map/ppermute | solution.py:47
  135.8 1.4 scatter_custom_fusion
  137.5 1.0 collective-permute-start.16
  140.8 2.2 collective-permute-done.17
  143.0 1.5 collective-permute-done.18
  145.5 1.1 collective-permute-start.21
  146.6 1.3 convert_reduce_fusion
  147.9 2.5 collective-permute-done.19
  150.4 1.6 collective-permute-done.20
  152.0 5.3 %collective-permute-done.21 = bf16[64,1536]{1,0:T(8,128)(2,1)S(1)} collective-permute-done((bf16[64,1536]{1,0:T(8,128)(2,1)S(1)}, bf16[64,1536]{1,0:T(8,128)(2,1)S(1)}, u32[]{:S(2)}, u32[]{:S(2)}) %collective-permute-start.21) | collective-permute-done | bytes 196640 | tf_op jit(solution)/shard_map/ppermute | solution.py:47
  158.4 4.5 %gather_fusion.2 = f32[512]{0:T(512)S(1)} fusion(f32[256,16]{0,1:T(8,128)S(1)} %fusion.92, s32[512]{0:T(512)S(1)} %reshape.381), kind=kCustom, calls=%fused_computation.2 | custom fusion | bytes 8192 | tf_op jit(solution)/shard_map/jit(take_along_axis)/gather | solution.py:260
  164.9 1.4 convolution_bitcast_fusion
  168.1 1.2 scatter_custom_fusion.1
  171.0 4.5 %collective-permute-done.23 = f32[64,768]{1,0:T(8,128)S(1)} collective-permute-done((f32[64,768]{1,0:T(8,128)S(1)}, f32[64,768]{1,0:T(8,128)S(1)}, u32[]{:S(2)}, u32[]{:S(2)}) %collective-permute-start.23) | collective-permute-done | bytes 196640 | tf_op jit(solution)/shard_map/ppermute | solution.py:47
  175.5 2.1 collective-permute-done.24
  177.6 5.3 %collective-permute-done.25 = f32[64,768]{1,0:T(8,128)} collective-permute-done((f32[64,768]{1,0:T(8,128)S(1)}, f32[64,768]{1,0:T(8,128)}, u32[]{:S(2)}, u32[]{:S(2)}) %collective-permute-start.25) | collective-permute-done | bytes 196640 | tf_op jit(solution)/shard_map/ppermute | solution.py:47
  182.9 1.0 add_add_fusion
  185.5 1.5 collective-permute-done.26
  187.0 1.8 collective-permute-done.27
  192.0 1.8 collective-permute-done.30
  194.6 5.5 %psum.7 = f32[4]{0:T(128)S(1)} all-reduce(f32[4]{0:T(128)S(1)} %get-tuple-element.10), channel_id=1, replica_groups=mesh['seq'=16,'row'=2,'col'=4] {'row'}, use_global_device_ids=true, to_apply=%region_14.15 | all-reduce | flops 4 | bytes 32 | tf_op jit(solution)/shard_map/psum | solution.py:144
  200.7 1.7 collective-permute-start.32
  203.2 3.2 %collective-permute-done.33 = bf16[4,768]{1,0:T(4,128)(2,1)S(1)} collective-permute-done((bf16[4,768]{1,0:T(4,128)(2,1)S(1)}, bf16[4,768]{1,0:T(4,128)(2,1)S(1)}, u32[]{:S(2)}, u32[]{:S(2)}) %collective-permute-start.33) | collective-permute-done | bytes 6176 | tf_op jit(solution)/shard_map/ppermute | solution.py:47
  206.8 1.8 collective-permute-start.35
  209.6 3.2 %collective-permute-done.36 = bf16[16,768]{1,0:T(8,128)(2,1)S(1)} collective-permute-done((bf16[16,768]{1,0:T(8,128)(2,1)S(1)}, bf16[16,768]{1,0:T(8,128)(2,1)S(1)}, u32[]{:S(2)}, u32[]{:S(2)}) %collective-permute-start.36) | collective-permute-done | bytes 24608 | tf_op jit(solution)/shard_map/ppermute | solution.py:47
  214.8 2.0 collective-permute-done.38
  216.8 1.9 collective-permute-done.39
  218.7 1.0 collective-permute-done.40
  221.3 5.2 %collective-permute-start.41 = (f32[128,1024]{1,0:T(8,128)}, f32[128,1024]{1,0:T(8,128)S(1)}, u32[]{:S(2)}, u32[]{:S(2)}) collective-permute-start(f32[128,1024]{1,0:T(8,128)} %constant_dynamic-slice_fusion), channel_id=1, source_target_pairs={{0,4},{4,0},{1,5},{5,1},{2,6},{6,2},{3,7},{7,3},{8,12},{12,8},{9,1... | collective-permute-start | bytes 1572872 | tf_op jit(solution)/shard_map/ppermute | solution.py:47
  226.6 1.7 collective-permute-done.41
  229.0 0.9 collective-permute-start.43
  231.2 1.8 collective-permute-done.43
  233.0 1.1 collective-permute-done.44
  234.6 0.9 collective-permute-start.46
  236.7 1.8 collective-permute-done.46
  239.2 1.3 collective-permute-start.48
  241.7 2.8 %collective-permute-done.49 = f32[1,384]{1,0:T(1,128)S(1)} collective-permute-done((f32[1,384]{1,0:T(1,128)S(1)}, f32[1,384]{1,0:T(1,128)S(1)}, u32[]{:S(2)}, u32[]{:S(2)}) %collective-permute-start.49) | collective-permute-done | bytes 1568 | tf_op jit(solution)/shard_map/ppermute | solution.py:47
  244.9 6.1 %all-gather.1 = f32[1,256]{1,0:T(1,128)S(1)} all-gather(f32[1,128]{1,0:T(1,128)S(1)} %fusion.56), channel_id=3, replica_groups=mesh['seq'=16,'row'=2,'col'=4] {'row'}, dimensions={1}, use_global_device_ids=true | all-gather | bytes 1536 | tf_op jit(solution)/shard_map/all_gather | solution.py:325
  (255 shorter events, 50.2 us)
Async XLA Ops:
  7.2 212.7 %copy-start = (bf16[768,1024]{1,0:T(8,128)(2,1)S(1)}, bf16[768,1024]{1,0:T(8,128)(2,1)}, u32[]{:S(2)}) copy-start(bf16[768,1024]{1,0:T(8,128)(2,1)} %param.28) | copy-start | bytes 4718596
  7.2 51.9 %all-gather.4.cloned.1.call-start = ((), (), s32[]{:S(2)}) async-start(), calls=%async_computation | async-start | bytes 1880064 | tf_op jit(solution)/shard_map/all_gather | solution.py:191
  9.9 8.9 %collective-permute-start.6 = (bf16[1,192,96]{2,1,0:T(8,128)(2,1)}, bf16[1,192,96]{2,1,0:T(8,128)(2,1)S(1)}, u32[]{:S(2)}, u32[]{:S(2)}) collective-permute-start(bf16[1,192,96]{2,1,0:T(8,128)(2,1)} %bitcast.68), channel_id=1, source_target_pairs={{0,24},{8,0},{16,8},{24,16},{32,56},{40,32},{48,40},{56,48},{64,88... | collective-permute-start | bytes 110600 | tf_op jit(solution)/shard_map/ppermute | solution.py:47
  14.6 4.8 %collective-permute-start.7 = (bf16[1,192,96]{2,1,0:T(8,128)(2,1)}, bf16[1,192,96]{2,1,0:T(8,128)(2,1)S(1)}, u32[]{:S(2)}, u32[]{:S(2)}) collective-permute-start(bf16[1,192,96]{2,1,0:T(8,128)(2,1)} %bitcast.69), channel_id=1, source_target_pairs={{0,16},{8,24},{16,0},{24,8},{32,48},{40,56},{48,32},{56,40},{64,80... | collective-permute-start | bytes 110600 | tf_op jit(solution)/shard_map/ppermute | solution.py:47
  14.6 4.9 %collective-permute-start.8 = (bf16[1,192,96]{2,1,0:T(8,128)(2,1)}, bf16[1,192,96]{2,1,0:T(8,128)(2,1)S(1)}, u32[]{:S(2)}, u32[]{:S(2)}) collective-permute-start(bf16[1,192,96]{2,1,0:T(8,128)(2,1)} %bitcast.70), channel_id=1, source_target_pairs={{0,8},{8,16},{16,24},{24,0},{32,40},{40,48},{48,56},{56,32},{64,72... | collective-permute-start | bytes 110600 | tf_op jit(solution)/shard_map/ppermute | solution.py:47
  20.3 37.9 %copy-start.10 = (bf16[1,192,96]{2,1,0:T(8,128)(2,1)}, bf16[1,192,96]{2,1,0:T(8,128)(2,1)S(1)}, u32[]{:S(2)}) copy-start(bf16[1,192,96]{2,1,0:T(8,128)(2,1)S(1)} %get-tuple-element.58) | copy-start | bytes 110596
  20.3 37.9 %copy-start.12 = (bf16[1,192,96]{2,1,0:T(8,128)(2,1)}, bf16[1,192,96]{2,1,0:T(8,128)(2,1)S(1)}, u32[]{:S(2)}) copy-start(bf16[1,192,96]{2,1,0:T(8,128)(2,1)S(1)} %get-tuple-element.59) | copy-start | bytes 110596
  20.3 37.9 %copy-start.14 = (bf16[1,192,96]{2,1,0:T(8,128)(2,1)}, bf16[1,192,96]{2,1,0:T(8,128)(2,1)S(1)}, u32[]{:S(2)}) copy-start(bf16[1,192,96]{2,1,0:T(8,128)(2,1)S(1)} %get-tuple-element.60) | copy-start | bytes 110596
  20.3 37.9 %copy-start.16 = (bf16[1,192,96]{2,1,0:T(8,128)(2,1)}, bf16[1,192,96]{2,1,0:T(8,128)(2,1)S(1)}, u32[]{:S(2)}) copy-start(bf16[1,192,96]{2,1,0:T(8,128)(2,1)S(1)} %get-tuple-element.61) | copy-start | bytes 110596
  20.4 37.7 %collective-permute-start.9 = (bf16[4,192,96]{2,1,0:T(8,128)(2,1)S(1)}, bf16[4,192,96]{2,1,0:T(8,128)(2,1)S(1)}, u32[]{:S(2)}, u32[]{:S(2)}) collective-permute-start(bf16[4,192,96]{2,1,0:T(8,128)(2,1)S(1)} %pad_maximum_fusion.2), channel_id=1, source_target_pairs={{0,96},{8,104},{16,112},{24,120},{32,0},{40,8},{48,16},{56,24},{64... | collective-permute-start | bytes 442376 | tf_op jit(solution)/shard_map/ppermute | solution.py:47
  23.2 34.9 %collective-permute-start.10 = (bf16[4,192,96]{2,1,0:T(8,128)(2,1)S(1)}, bf16[4,192,96]{2,1,0:T(8,128)(2,1)S(1)}, u32[]{:S(2)}, u32[]{:S(2)}) collective-permute-start(bf16[4,192,96]{2,1,0:T(8,128)(2,1)S(1)} %pad_maximum_fusion.2), channel_id=1, source_target_pairs={{0,64},{8,72},{16,80},{24,88},{32,96},{40,104},{48,112},{56,120},{... | collective-permute-start | bytes 442376 | tf_op jit(solution)/shard_map/ppermute | solution.py:47
  23.6 34.6 %collective-permute-start.11 = (bf16[4,192,96]{2,1,0:T(8,128)(2,1)S(1)}, bf16[4,192,96]{2,1,0:T(8,128)(2,1)S(1)}, u32[]{:S(2)}, u32[]{:S(2)}) collective-permute-start(bf16[4,192,96]{2,1,0:T(8,128)(2,1)S(1)} %pad_maximum_fusion.2), channel_id=1, source_target_pairs={{0,32},{8,40},{16,48},{24,56},{32,64},{40,72},{48,80},{56,88},{64,... | collective-permute-start | bytes 442376 | tf_op jit(solution)/shard_map/ppermute | solution.py:47
  24.4 32.6 %copy-start.25 = (f32[1536]{0:T(1024)S(1)}, f32[1536]{0:T(1024)}, u32[]{:S(2)}) copy-start(f32[1536]{0:T(1024)} %param.16) | copy-start | bytes 18436
  97.2 17.5 %copy-start.2 = (bf16[4,192,96]{2,1,0:T(8,128)(2,1)S(1)}, bf16[4,192,96]{2,1,0:T(8,128)(2,1)}, u32[]{:S(2)}) copy-start(bf16[4,192,96]{2,1,0:T(8,128)(2,1)} %get-tuple-element.36) | copy-start | bytes 442372
  101.6 35.6 %copy-start.19 = (bf16[16,1536]{1,0:T(8,128)(2,1)S(1)}, bf16[16,1536]{1,0:T(8,128)(2,1)}, u32[]{:S(2)}) copy-start(bf16[16,1536]{1,0:T(8,128)(2,1)} %param.15) | copy-start | bytes 147460
  102.7 3.4 %collective-permute-start = (f32[16,792]{1,0:T(8,128)S(1)}, f32[16,792]{1,0:T(8,128)S(1)}, u32[]{:S(2)}, u32[]{:S(2)}) collective-permute-start(f32[16,792]{1,0:T(8,128)S(1)} %get-tuple-element.50), channel_id=1, source_target_pairs={{0,96},{8,104},{16,112},{24,120},{32,0},{40,8},{48,16},{56,24},{64... | collective-permute-start | bytes 152072 | tf_op jit(solution)/shard_map/ppermute | solution.py:47
  104.8 4.6 %collective-permute-start.1 = (f32[16,792]{1,0:T(8,128)S(1)}, f32[16,792]{1,0:T(8,128)S(1)}, u32[]{:S(2)}, u32[]{:S(2)}) collective-permute-start(f32[16,792]{1,0:T(8,128)S(1)} %get-tuple-element.49), channel_id=1, source_target_pairs={{0,64},{8,72},{16,80},{24,88},{32,96},{40,104},{48,112},{56,120},{... | collective-permute-start | bytes 152072 | tf_op jit(solution)/shard_map/ppermute | solution.py:47
  105.3 4.7 %collective-permute-start.2 = (f32[16,792]{1,0:T(8,128)S(1)}, f32[16,792]{1,0:T(8,128)S(1)}, u32[]{:S(2)}, u32[]{:S(2)}) collective-permute-start(f32[16,792]{1,0:T(8,128)S(1)} %get-tuple-element.48), channel_id=1, source_target_pairs={{0,32},{8,40},{16,48},{24,56},{32,64},{40,72},{48,80},{56,88},{64,... | collective-permute-start | bytes 152072 | tf_op jit(solution)/shard_map/ppermute | solution.py:47
  106.0 31.4 %copy-start.21 = (f32[1536]{0:T(1024)S(1)}, f32[1536]{0:T(1024)}, u32[]{:S(2)}) copy-start(f32[1536]{0:T(1024)} %param.22) | copy-start | bytes 18436
  111.4 46.2 %copy-start.20 = (f32[1536,16]{0,1:T(8,128)S(1)}, f32[1536,16]{0,1:T(8,128)}, u32[]{:S(2)}) copy-start(f32[1536,16]{0,1:T(8,128)} %param.23) | copy-start | bytes 294916
  111.5 4.8 %collective-permute-start.3 = (f32[4,792]{1,0:T(4,128)S(1)}, f32[4,792]{1,0:T(4,128)S(1)}, u32[]{:S(2)}, u32[]{:S(2)}) collective-permute-start(f32[4,792]{1,0:T(4,128)S(1)} %get-tuple-element.74), channel_id=1, source_target_pairs={{0,24},{8,0},{16,8},{24,16},{32,56},{40,32},{48,40},{56,48},{64,88... | collective-permute-start | bytes 38024 | tf_op jit(solution)/shard_map/ppermute | solution.py:47
  113.4 4.1 %collective-permute-start.4 = (f32[4,792]{1,0:T(4,128)S(1)}, f32[4,792]{1,0:T(4,128)S(1)}, u32[]{:S(2)}, u32[]{:S(2)}) collective-permute-start(f32[4,792]{1,0:T(4,128)S(1)} %get-tuple-element.73), channel_id=1, source_target_pairs={{0,16},{8,24},{16,0},{24,8},{32,48},{40,56},{48,32},{56,40},{64,80... | collective-permute-start | bytes 38024 | tf_op jit(solution)/shard_map/ppermute | solution.py:47
  114.6 3.8 %collective-permute-start.5 = (f32[4,792]{1,0:T(4,128)S(1)}, f32[4,792]{1,0:T(4,128)S(1)}, u32[]{:S(2)}, u32[]{:S(2)}) collective-permute-start(f32[4,792]{1,0:T(4,128)S(1)} %get-tuple-element.72), channel_id=1, source_target_pairs={{0,8},{8,16},{16,24},{24,0},{32,40},{40,48},{48,56},{56,32},{64,72... | collective-permute-start | bytes 38024 | tf_op jit(solution)/shard_map/ppermute | solution.py:47
  119.6 4.4 %collective-permute-start.12 = (f32[16,1536]{1,0:T(8,128)S(1)}, f32[16,1536]{1,0:T(8,128)S(1)}, u32[]{:S(2)}, u32[]{:S(2)}) collective-permute-start(f32[16,1536]{1,0:T(8,128)S(1)} %fusion.91), channel_id=1, source_target_pairs={{0,3},{1,0},{2,1},{3,2},{4,7},{5,4},{6,5},{7,6},{8,11},{9,8},{10,9... | collective-permute-start | bytes 294920 | tf_op jit(solution)/shard_map/ppermute | solution.py:47
  122.1 5.1 %collective-permute-start.13 = (f32[16,1536]{1,0:T(8,128)S(1)}, f32[16,1536]{1,0:T(8,128)S(1)}, u32[]{:S(2)}, u32[]{:S(2)}) collective-permute-start(f32[16,1536]{1,0:T(8,128)S(1)} %fusion.91), channel_id=1, source_target_pairs={{0,2},{1,3},{2,0},{3,1},{4,6},{5,7},{6,4},{7,5},{8,10},{9,11},{10,... | collective-permute-start | bytes 294920 | tf_op jit(solution)/shard_map/ppermute | solution.py:47
  122.6 5.5 %collective-permute-start.14 = (f32[16,1536]{1,0:T(8,128)S(1)}, f32[16,1536]{1,0:T(8,128)S(1)}, u32[]{:S(2)}, u32[]{:S(2)}) collective-permute-start(f32[16,1536]{1,0:T(8,128)S(1)} %fusion.91), channel_id=1, source_target_pairs={{0,1},{1,2},{2,3},{3,0},{4,5},{5,6},{6,7},{7,4},{8,9},{9,10},{10,1... | collective-permute-start | bytes 294920 | tf_op jit(solution)/shard_map/ppermute | solution.py:47
  128.1 9.1 %collective-permute-start.15 = (f32[16,1536]{1,0:T(8,128)S(1)}, f32[16,1536]{1,0:T(8,128)S(1)}, u32[]{:S(2)}, u32[]{:S(2)}) collective-permute-start(f32[16,1536]{1,0:T(8,128)S(1)} %add_add_fusion.2), channel_id=1, source_target_pairs={{0,4},{1,5},{2,6},{3,7},{4,0},{5,1},{6,2},{7,3},{8,12},{9,13},{10,... | collective-permute-start | bytes 294920 | tf_op jit(solution)/shard_map/ppermute | solution.py:47
  137.5 3.4 %collective-permute-start.16 = (bf16[16,1536]{1,0:T(8,128)(2,1)S(1)}, bf16[16,1536]{1,0:T(8,128)(2,1)S(1)}, u32[]{:S(2)}, u32[]{:S(2)}) collective-permute-start(bf16[16,1536]{1,0:T(8,128)(2,1)S(1)} %multiply_convert_fusion), channel_id=1, source_target_pairs={{0,24},{8,0},{16,8},{24,16},{32,56},{40,32},{48,40},{56,48},{64,88... | collective-permute-start | bytes 147464 | tf_op jit(solution)/shard_map/ppermute | solution.py:47
  138.5 4.5 %collective-permute-start.17 = (bf16[16,1536]{1,0:T(8,128)(2,1)S(1)}, bf16[16,1536]{1,0:T(8,128)(2,1)S(1)}, u32[]{:S(2)}, u32[]{:S(2)}) collective-permute-start(bf16[16,1536]{1,0:T(8,128)(2,1)S(1)} %multiply_convert_fusion), channel_id=1, source_target_pairs={{0,16},{8,24},{16,0},{24,8},{32,48},{40,56},{48,32},{56,40},{64,80... | collective-permute-start | bytes 147464 | tf_op jit(solution)/shard_map/ppermute | solution.py:47
  139.1 5.3 %collective-permute-start.18 = (bf16[16,1536]{1,0:T(8,128)(2,1)S(1)}, bf16[16,1536]{1,0:T(8,128)(2,1)S(1)}, u32[]{:S(2)}, u32[]{:S(2)}) collective-permute-start(bf16[16,1536]{1,0:T(8,128)(2,1)S(1)} %multiply_convert_fusion), channel_id=1, source_target_pairs={{0,8},{8,16},{16,24},{24,0},{32,40},{40,48},{48,56},{56,32},{64,72... | collective-permute-start | bytes 147464 | tf_op jit(solution)/shard_map/ppermute | solution.py:47
  144.6 5.8 %collective-permute-start.19 = (bf16[64,1536]{1,0:T(8,128)(2,1)S(1)}, bf16[64,1536]{1,0:T(8,128)(2,1)S(1)}, u32[]{:S(2)}, u32[]{:S(2)}) collective-permute-start(bf16[64,1536]{1,0:T(8,128)(2,1)S(1)} %pad_maximum_fusion.3), channel_id=1, source_target_pairs={{0,96},{8,104},{16,112},{24,120},{32,0},{40,8},{48,16},{56,24},{64... | collective-permute-start | bytes 589832 | tf_op jit(solution)/shard_map/ppermute | solution.py:47
  144.7 7.3 %collective-permute-start.20 = (bf16[64,1536]{1,0:T(8,128)(2,1)S(1)}, bf16[64,1536]{1,0:T(8,128)(2,1)S(1)}, u32[]{:S(2)}, u32[]{:S(2)}) collective-permute-start(bf16[64,1536]{1,0:T(8,128)(2,1)S(1)} %pad_maximum_fusion.3), channel_id=1, source_target_pairs={{0,64},{8,72},{16,80},{24,88},{32,96},{40,104},{48,112},{56,120},{... | collective-permute-start | bytes 589832 | tf_op jit(solution)/shard_map/ppermute | solution.py:47
  145.5 11.8 %collective-permute-start.21 = (bf16[64,1536]{1,0:T(8,128)(2,1)S(1)}, bf16[64,1536]{1,0:T(8,128)(2,1)S(1)}, u32[]{:S(2)}, u32[]{:S(2)}) collective-permute-start(bf16[64,1536]{1,0:T(8,128)(2,1)S(1)} %pad_maximum_fusion.3), channel_id=1, source_target_pairs={{0,32},{8,40},{16,48},{24,56},{32,64},{40,72},{48,80},{56,88},{64,... | collective-permute-start | bytes 589832 | tf_op jit(solution)/shard_map/ppermute | solution.py:47
  163.0 28.1 %copy-start.26 = (f32[1536]{0:T(1024)S(1)}, f32[1536]{0:T(1024)}, u32[]{:S(2)}) copy-start(f32[1536]{0:T(1024)} %param.27) | copy-start | bytes 18436
  164.9 61.6 %copy-start.28 = (s32[256]{0:T(256)S(1)}, s32[256]{0:T(256)}, u32[]{:S(2)}) copy-start(s32[256]{0:T(256)} %param.29) | copy-start | bytes 3076
  166.3 1.6 collective-permute-start.22
  169.4 6.2 %collective-permute-start.23 = (f32[64,768]{1,0:T(8,128)S(1)}, f32[64,768]{1,0:T(8,128)S(1)}, u32[]{:S(2)}, u32[]{:S(2)}) collective-permute-start(f32[64,768]{1,0:T(8,128)S(1)} %get-tuple-element.31), channel_id=1, source_target_pairs={{0,96},{1,97},{2,98},{3,99},{8,104},{9,105},{10,106},{11,107},{16,... | collective-permute-start | bytes 589832 | tf_op jit(solution)/shard_map/ppermute | solution.py:47
  170.2 7.4 %collective-permute-start.24 = (f32[64,768]{1,0:T(8,128)S(1)}, f32[64,768]{1,0:T(8,128)S(1)}, u32[]{:S(2)}, u32[]{:S(2)}) collective-permute-start(f32[64,768]{1,0:T(8,128)S(1)} %get-tuple-element.30), channel_id=1, source_target_pairs={{0,64},{1,65},{2,66},{3,67},{8,72},{9,73},{10,74},{11,75},{16,80},... | collective-permute-start | bytes 589832 | tf_op jit(solution)/shard_map/ppermute | solution.py:47
  170.5 12.4 %collective-permute-start.25 = (f32[64,768]{1,0:T(8,128)S(1)}, f32[64,768]{1,0:T(8,128)}, u32[]{:S(2)}, u32[]{:S(2)}) collective-permute-start(f32[64,768]{1,0:T(8,128)S(1)} %get-tuple-element.29), channel_id=1, source_target_pairs={{0,32},{1,33},{2,34},{3,35},{8,40},{9,41},{10,42},{11,43},{16,48},... | collective-permute-start | bytes 589832 | tf_op jit(solution)/shard_map/ppermute | solution.py:47
  184.0 3.0 %collective-permute-start.26 = (f32[16,768]{1,0:T(8,128)S(1)}, f32[16,768]{1,0:T(8,128)S(1)}, u32[]{:S(2)}, u32[]{:S(2)}) collective-permute-start(f32[16,768]{1,0:T(8,128)S(1)} %get-tuple-element.53), channel_id=1, source_target_pairs={{0,24},{1,25},{2,26},{3,27},{8,0},{9,1},{10,2},{11,3},{16,8},{17,9... | collective-permute-start | bytes 147464 | tf_op jit(solution)/shard_map/ppermute | solution.py:47
  184.3 4.4 %collective-permute-start.27 = (f32[16,768]{1,0:T(8,128)S(1)}, f32[16,768]{1,0:T(8,128)S(1)}, u32[]{:S(2)}, u32[]{:S(2)}) collective-permute-start(f32[16,768]{1,0:T(8,128)S(1)} %get-tuple-element.52), channel_id=1, source_target_pairs={{0,16},{1,17},{2,18},{3,19},{8,24},{9,25},{10,26},{11,27},{16,0},{... | collective-permute-start | bytes 147464 | tf_op jit(solution)/shard_map/ppermute | solution.py:47
  184.8 4.6 %collective-permute-start.28 = (f32[16,768]{1,0:T(8,128)S(1)}, f32[16,768]{1,0:T(8,128)S(1)}, u32[]{:S(2)}, u32[]{:S(2)}) collective-permute-start(f32[16,768]{1,0:T(8,128)S(1)} %get-tuple-element.51), channel_id=1, source_target_pairs={{0,8},{1,9},{2,10},{3,11},{8,16},{9,17},{10,18},{11,19},{16,24},{1... | collective-permute-start | bytes 147464 | tf_op jit(solution)/shard_map/ppermute | solution.py:47
  189.4 2.6 %collective-permute-start.29 = (f32[4,768]{1,0:T(4,128)S(1)}, f32[4,768]{1,0:T(4,128)S(1)}, u32[]{:S(2)}, u32[]{:S(2)}) collective-permute-start(f32[4,768]{1,0:T(4,128)S(1)} %get-tuple-element.77), channel_id=1, source_target_pairs={{0,3},{1,0},{2,1},{3,2},{8,11},{9,8},{10,9},{11,10},{16,19},{17,16... | collective-permute-start | bytes 36872 | tf_op jit(solution)/shard_map/ppermute | solution.py:47
  189.8 4.0 %collective-permute-start.30 = (f32[4,768]{1,0:T(4,128)S(1)}, f32[4,768]{1,0:T(4,128)S(1)}, u32[]{:S(2)}, u32[]{:S(2)}) collective-permute-start(f32[4,768]{1,0:T(4,128)S(1)} %get-tuple-element.76), channel_id=1, source_target_pairs={{0,2},{1,3},{2,0},{3,1},{8,10},{9,11},{10,8},{11,9},{16,18},{17,19... | collective-permute-start | bytes 36872 | tf_op jit(solution)/shard_map/ppermute | solution.py:47
  190.3 4.1 %collective-permute-start.31 = (f32[4,768]{1,0:T(4,128)S(1)}, f32[4,768]{1,0:T(4,128)S(1)}, u32[]{:S(2)}, u32[]{:S(2)}) collective-permute-start(f32[4,768]{1,0:T(4,128)S(1)} %get-tuple-element.75), channel_id=1, source_target_pairs={{0,1},{1,2},{2,3},{3,0},{8,9},{9,10},{10,11},{11,8},{16,17},{17,18... | collective-permute-start | bytes 36872 | tf_op jit(solution)/shard_map/ppermute | solution.py:47
  200.7 2.5 collective-permute-start.32
  202.5 4.0 %collective-permute-start.33 = (bf16[4,768]{1,0:T(4,128)(2,1)S(1)}, bf16[4,768]{1,0:T(4,128)(2,1)S(1)}, u32[]{:S(2)}, u32[]{:S(2)}) collective-permute-start(bf16[4,768]{1,0:T(4,128)(2,1)S(1)} %get-tuple-element.82), channel_id=1, source_target_pairs={{0,2},{1,3},{2,0},{3,1},{8,10},{9,11},{10,8},{11,9},{16,18},{17,19... | collective-permute-start | bytes 18440 | tf_op jit(solution)/shard_map/ppermute | solution.py:47
  203.1 3.7 %collective-permute-start.34 = (bf16[4,768]{1,0:T(4,128)(2,1)S(1)}, bf16[4,768]{1,0:T(4,128)(2,1)S(1)}, u32[]{:S(2)}, u32[]{:S(2)}) collective-permute-start(bf16[4,768]{1,0:T(4,128)(2,1)S(1)} %get-tuple-element.82), channel_id=1, source_target_pairs={{0,1},{1,2},{2,3},{3,0},{8,9},{9,10},{10,11},{11,8},{16,17},{17,18... | collective-permute-start | bytes 18440 | tf_op jit(solution)/shard_map/ppermute | solution.py:47
  206.8 2.8 %collective-permute-start.35 = (bf16[16,768]{1,0:T(8,128)(2,1)S(1)}, bf16[16,768]{1,0:T(8,128)(2,1)S(1)}, u32[]{:S(2)}, u32[]{:S(2)}) collective-permute-start(bf16[16,768]{1,0:T(8,128)(2,1)S(1)} %pad_maximum_fusion.8), channel_id=1, source_target_pairs={{0,24},{1,25},{2,26},{3,27},{8,0},{9,1},{10,2},{11,3},{16,8},{17,9... | collective-permute-start | bytes 73736 | tf_op jit(solution)/shard_map/ppermute | solution.py:47
  208.7 4.2 %collective-permute-start.36 = (bf16[16,768]{1,0:T(8,128)(2,1)S(1)}, bf16[16,768]{1,0:T(8,128)(2,1)S(1)}, u32[]{:S(2)}, u32[]{:S(2)}) collective-permute-start(bf16[16,768]{1,0:T(8,128)(2,1)S(1)} %pad_maximum_fusion.8), channel_id=1, source_target_pairs={{0,16},{1,17},{2,18},{3,19},{8,24},{9,25},{10,26},{11,27},{16,0},{... | collective-permute-start | bytes 73736 | tf_op jit(solution)/shard_map/ppermute | solution.py:47
  209.3 3.9 %collective-permute-start.37 = (bf16[16,768]{1,0:T(8,128)(2,1)S(1)}, bf16[16,768]{1,0:T(8,128)(2,1)S(1)}, u32[]{:S(2)}, u32[]{:S(2)}) collective-permute-start(bf16[16,768]{1,0:T(8,128)(2,1)S(1)} %pad_maximum_fusion.8), channel_id=1, source_target_pairs={{0,8},{1,9},{2,10},{3,11},{8,16},{9,17},{10,18},{11,19},{16,24},{1... | collective-permute-start | bytes 73736 | tf_op jit(solution)/shard_map/ppermute | solution.py:47
  213.3 3.5 %collective-permute-start.38 = (bf16[64,768]{1,0:T(8,128)(2,1)S(1)}, bf16[64,768]{1,0:T(8,128)(2,1)S(1)}, u32[]{:S(2)}, u32[]{:S(2)}) collective-permute-start(bf16[64,768]{1,0:T(8,128)(2,1)S(1)} %pad_maximum_fusion.5), channel_id=1, source_target_pairs={{0,96},{1,97},{2,98},{3,99},{8,104},{9,105},{10,106},{11,107},{16,... | collective-permute-start | bytes 294920 | tf_op jit(solution)/shard_map/ppermute | solution.py:47
  213.7 5.0 %collective-permute-start.39 = (bf16[64,768]{1,0:T(8,128)(2,1)S(1)}, bf16[64,768]{1,0:T(8,128)(2,1)S(1)}, u32[]{:S(2)}, u32[]{:S(2)}) collective-permute-start(bf16[64,768]{1,0:T(8,128)(2,1)S(1)} %pad_maximum_fusion.5), channel_id=1, source_target_pairs={{0,64},{1,65},{2,66},{3,67},{8,72},{9,73},{10,74},{11,75},{16,80},... | collective-permute-start | bytes 294920 | tf_op jit(solution)/shard_map/ppermute | solution.py:47
  213.9 5.8 %collective-permute-start.40 = (bf16[64,768]{1,0:T(8,128)(2,1)S(1)}, bf16[64,768]{1,0:T(8,128)(2,1)S(1)}, u32[]{:S(2)}, u32[]{:S(2)}) collective-permute-start(bf16[64,768]{1,0:T(8,128)(2,1)S(1)} %pad_maximum_fusion.5), channel_id=1, source_target_pairs={{0,32},{1,33},{2,34},{3,35},{8,40},{9,41},{10,42},{11,43},{16,48},... | collective-permute-start | bytes 294920 | tf_op jit(solution)/shard_map/ppermute | solution.py:47
  221.3 6.9 %collective-permute-start.41 = (f32[128,1024]{1,0:T(8,128)}, f32[128,1024]{1,0:T(8,128)S(1)}, u32[]{:S(2)}, u32[]{:S(2)}) collective-permute-start(f32[128,1024]{1,0:T(8,128)} %constant_dynamic-slice_fusion), channel_id=1, source_target_pairs={{0,4},{4,0},{1,5},{5,1},{2,6},{6,2},{3,7},{7,3},{8,12},{12,8},{9,1... | collective-permute-start | bytes 1572872 | tf_op jit(solution)/shard_map/ppermute | solution.py:47
  228.7 2.5 collective-permute-start.42
  229.0 3.9 %collective-permute-start.43 = (f32[1,384]{1,0:T(1,128)S(1)}, f32[1,384]{1,0:T(1,128)S(1)}, u32[]{:S(2)}, u32[]{:S(2)}) collective-permute-start(f32[1,384]{1,0:T(1,128)S(1)} %pad_maximum_fusion.9), channel_id=1, source_target_pairs={{0,2},{1,3},{2,0},{3,1},{8,10},{9,11},{10,8},{11,9},{16,18},{17,19... | collective-permute-start | bytes 4616 | tf_op jit(solution)/shard_map/ppermute | solution.py:47
  230.0 4.1 %collective-permute-start.44 = (f32[1,384]{1,0:T(1,128)S(1)}, f32[1,384]{1,0:T(1,128)S(1)}, u32[]{:S(2)}, u32[]{:S(2)}) collective-permute-start(f32[1,384]{1,0:T(1,128)S(1)} %pad_maximum_fusion.9), channel_id=1, source_target_pairs={{0,1},{1,2},{2,3},{3,0},{8,9},{9,10},{10,11},{11,8},{16,17},{17,18... | collective-permute-start | bytes 4616 | tf_op jit(solution)/shard_map/ppermute | solution.py:47
  234.2 2.5 collective-permute-start.45
  234.6 3.9 %collective-permute-start.46 = (f32[1,384]{1,0:T(1,128)S(1)}, f32[1,384]{1,0:T(1,128)S(1)}, u32[]{:S(2)}, u32[]{:S(2)}) collective-permute-start(f32[1,384]{1,0:T(1,128)S(1)} %pad_maximum_fusion.10), channel_id=1, source_target_pairs={{0,16},{1,17},{2,18},{3,19},{8,24},{9,25},{10,26},{11,27},{16,0},{... | collective-permute-start | bytes 4616 | tf_op jit(solution)/shard_map/ppermute | solution.py:47
  235.5 3.6 %collective-permute-start.47 = (f32[1,384]{1,0:T(1,128)S(1)}, f32[1,384]{1,0:T(1,128)S(1)}, u32[]{:S(2)}, u32[]{:S(2)}) collective-permute-start(f32[1,384]{1,0:T(1,128)S(1)} %pad_maximum_fusion.10), channel_id=1, source_target_pairs={{0,8},{1,9},{2,10},{3,11},{8,16},{9,17},{10,18},{11,19},{16,24},{1... | collective-permute-start | bytes 4616 | tf_op jit(solution)/shard_map/ppermute | solution.py:47
  239.2 2.5 collective-permute-start.48
  240.5 3.9 %collective-permute-start.49 = (f32[1,384]{1,0:T(1,128)S(1)}, f32[1,384]{1,0:T(1,128)S(1)}, u32[]{:S(2)}, u32[]{:S(2)}) collective-permute-start(f32[1,384]{1,0:T(1,128)S(1)} %pad_maximum_fusion.11), channel_id=1, source_target_pairs={{0,64},{1,65},{2,66},{3,67},{8,72},{9,73},{10,74},{11,75},{16,80},... | collective-permute-start | bytes 4616 | tf_op jit(solution)/shard_map/ppermute | solution.py:47
  241.2 3.6 %collective-permute-start.50 = (f32[1,384]{1,0:T(1,128)S(1)}, f32[1,384]{1,0:T(1,128)S(1)}, u32[]{:S(2)}, u32[]{:S(2)}) collective-permute-start(f32[1,384]{1,0:T(1,128)S(1)} %pad_maximum_fusion.11), channel_id=1, source_target_pairs={{0,32},{1,33},{2,34},{3,35},{8,40},{9,41},{10,42},{11,43},{16,48},... | collective-permute-start | bytes 4616 | tf_op jit(solution)/shard_map/ppermute | solution.py:47
  (17 other events, 121.7 us)
Sparse Core Ops, SparseCore 0:
  10.2 48.2 all-gather.3

commit v2 on v1

--- a/solution.py
+++ b/solution.py
@@ -184,7 +184,8 @@
     block_index = lax.axis_index(("seq", "col"))
     own_count = hidden_in.shape[0]
     block_start = seq_index * own_count
-    pieces = [hidden_in.reshape(-1), jnp.concatenate([w_query, w_keyval], axis=1).reshape(-1)]
+    own_normed_in = rms_scale(hidden_in.astype(jnp.float32), attn_gain).astype(jnp.bfloat16)
+    pieces = [own_normed_in.reshape(-1), jnp.concatenate([w_query, w_keyval], axis=1).reshape(-1)]
     bounds = [0]
     for piece in pieces:
         bounds.append(bounds[-1] + piece.shape[0])
@@ -202,8 +203,7 @@
     width = every_row.shape[1]
     half = width // lax.axis_size("row")
     col_start = row_index * half
-    state_in = every_row.astype(jnp.float32)
-    normed_in = rms_scale(state_in, attn_gain).astype(jnp.bfloat16)
+    normed_in = every_row
     query_cols = w_query.shape[1]
     group = query_cols // HD
     both = jnp.dot(normed_in, w_both_all, preferred_element_type=jnp.float32)

time: 263 us -> 256 us (0.973)
  local copies, waits for them, and re-layouts: 59.9 us -> 54.5 us
    mul x4 -> x0, local copies, waits for them, and re-layouts: 3.02 us -> none  [the longest x1 2.82 us: rms_scale(): mean_square = jnp.mean(values * values, axis=-1, keepdims=True)]
    unnamed x61 -> x58, local copies, waits for them, and re-layouts: 34.2 us -> 31.8 us
  transfers between devices with their start and end apart: 52 -> 52, of which waited for: 43 -> 45; matrix products, arithmetic and copies ran while one was open for 18% -> 18% of each run, Pallas kernels for 0% -> 0%
where the time goes in v2:
time: 256 us; the launch traced here: 252 us
  waiting for transfers between devices  68.5 us (27%)
  local copies, waits for them, and re-layouts  54.5 us (21%)
  starting transfers between devices  53.5 us (21%)
  matrix products  25.9 us (10%)
  other arithmetic  22.5 us (9%)
  between operations  15.4 us (6%)
  blocking collectives  12 us (5%)
    ppermute x51, waiting for transfers between devices, group_exchange(): received.append(lax.ppermute(sent, axes, pairs))  67.7 us
    ppermute x51, starting transfers between devices, group_exchange(): received.append(lax.ppermute(sent, axes, pairs))  53.5 us
    unnamed x58, local copies, waits for them, and re-layouts  31.8 us
    dot_general x1, matrix products, on_device(): jnp.einsum('rqp,rpd->rqd', old_weights, cached_values, precision=lax.Prec...  12.9 us
    dot_general x1, matrix products, on_device(): jnp.einsum('rqd,rpd->rqp', queries, cached_keys, precision=lax.Precision....  8.29 us
    all_gather x1, blocking collectives, on_device(): logprob = lax.all_gather(logprob_part, 'row', axis=0, tiled=True)  6.49 us
    gather x5, local copies, waits for them, and re-layouts, on_device(): chosen = jnp.take_along_axis(router, routes, axis=1)  5.71 us
    psum x1, blocking collectives, final_scale(): squares = lax.psum(jnp.sum(state * state, axis=-1), 'row')  5.5 us
  transfers between devices with their start and end apart: 52, of which 45 were waited for; matrix products, arithmetic and copies ran while one was open for 18% of the time, Pallas kernels for 0%

profile of v2, /device:TPU:1, one launch (start us, length us, event | category | flops | bytes accessed | tf_op | source)
XLA Modules:
  0.0 252.2 jit_solution(13044286266933897268)
XLA Ops:
  7.2 1.0 pad_maximum_fusion.6
  8.4 0.9 fusion.22
  9.3 0.9 fusion.24
  11.0 4.6 %collective-permute-start.6 = (bf16[1,192,96]{2,1,0:T(8,128)(2,1)}, bf16[1,192,96]{2,1,0:T(8,128)(2,1)S(1)}, u32[]{:S(2)}, u32[]{:S(2)}) collective-permute-start(bf16[1,192,96]{2,1,0:T(8,128)(2,1)} %bitcast.64), channel_id=1, source_target_pairs={{0,24},{8,0},{16,8},{24,16},{32,56},{40,32},{48,40},{56,48},{64,88... | collective-permute-start | bytes 110600 | tf_op jit(solution)/shard_map/ppermute | solution.py:47
  17.1 1.3 bitcast_or_fusion
  18.3 1.4 broadcast_compare_fusion
  21.4 2.8 %collective-permute-start.9 = (bf16[4,192,96]{2,1,0:T(8,128)(2,1)S(1)}, bf16[4,192,96]{2,1,0:T(8,128)(2,1)S(1)}, u32[]{:S(2)}, u32[]{:S(2)}) collective-permute-start(bf16[4,192,96]{2,1,0:T(8,128)(2,1)S(1)} %pad_maximum_fusion.2), channel_id=1, source_target_pairs={{0,96},{8,104},{16,112},{24,120},{32,0},{40,8},{48,16},{56,24},{64... | collective-permute-start | bytes 442376 | tf_op jit(solution)/shard_map/ppermute | solution.py:47
  25.5 31.1 %copy.59 = bf16[64,1536,128]{1,2,0:T(8,128)(2,1)} copy(bf16[64,1536,128]{2,1,0:T(8,128)(2,1)} %param.20) | data formatting | bytes 50331648 | tf_op args[5]
  57.7 0.9 select_select_fusion.7
  59.4 1.9 reshape.393
  61.4 1.0 slice.296
  62.3 1.0 slice.297
  63.3 1.5 reshape.339
  64.8 2.5 reshape.340
  68.6 8.3 %fusion.2 = (f32[64,12]{1,0:T(8,128)S(1)}, f32[64,12,1536]{2,1,0:T(8,128)S(1)}) fusion(pred[64,1536]{1,0:T(8,128)(4,1)} %broadcast_compare_fusion, f32[64,12,64]{2,1,0:T(8,128)S(1)} %reshape.341, bf16[64,1536,2,64]{1,3,2,0:T(8,128)(2,1)} %bitcast.61), kind=kOutput, calls=%fused_computation.11 | convolution fusion | flops 909507840 | bytes 17599488 | tf_op jit(solution)/shard_map/rqd,rpd->rqp/dot_general | solution.py:220
  77.4 12.9 %fusion = f32[64,12,64]{2,1,0:T(8,128)S(1)} fusion(bf16[64,1536,2,64]{1,3,2,0:T(8,128)(2,1)} %bitcast.62, f32[64,12,1536]{2,1,0:T(8,128)S(1)} %get-tuple-element.99, f32[64,12]{1,0:T(8,128)S(1)} %max.52, pred[64,1536]{1,0:T(8,128)(4,1)S(1)} %copy-done.1), kind=kOutput, calls=%fused_computation.6 | convolution fusion | flops 910688256 | bytes 17599488 | tf_op jit(solution)/shard_map/rqp,rpd->rqd/dot_general | solution.py:239
  90.4 2.8 %fusion.3 = f32[64,12]{1,0:T(8,128)} fusion(f32[64,12,1536]{2,1,0:T(8,128)S(1)} %get-tuple-element.99, f32[64,12]{1,0:T(8,128)S(1)} %max.52, pred[64,1536]{1,0:T(8,128)(4,1)S(1)} %copy-done.1), kind=kLoop, calls=%fused_computation.12 | loop fusion | flops 5897472 | bytes 4823040 | tf_op jit(solution)/shard_map/reduce_sum | solution.py:238
  95.7 2.6 %collective-permute-start = (f32[16,792]{1,0:T(8,128)S(1)}, f32[16,792]{1,0:T(8,128)S(1)}, u32[]{:S(2)}, u32[]{:S(2)}) collective-permute-start(f32[16,792]{1,0:T(8,128)S(1)} %get-tuple-element.50), channel_id=1, source_target_pairs={{0,96},{8,104},{16,112},{24,120},{32,0},{40,8},{48,16},{56,24},{64... | collective-permute-start | bytes 152072 | tf_op jit(solution)/shard_map/ppermute | solution.py:47
  99.6 3.3 %collective-permute-done.1 = f32[16,792]{1,0:T(8,128)S(1)} collective-permute-done((f32[16,792]{1,0:T(8,128)S(1)}, f32[16,792]{1,0:T(8,128)S(1)}, u32[]{:S(2)}, u32[]{:S(2)}) %collective-permute-start.1) | collective-permute-done | bytes 50720 | tf_op jit(solution)/shard_map/ppermute | solution.py:47
  105.0 1.1 collective-permute-start.3
  106.2 1.7 collective-permute-start.4
  108.6 0.9 reshape.349
  110.2 1.4 collective-permute-done.5
  112.8 2.6 %collective-permute-start.12 = (f32[16,1536]{1,0:T(8,128)S(1)}, f32[16,1536]{1,0:T(8,128)S(1)}, u32[]{:S(2)}, u32[]{:S(2)}) collective-permute-start(f32[16,1536]{1,0:T(8,128)S(1)} %fusion.92), channel_id=1, source_target_pairs={{0,3},{1,0},{2,1},{3,2},{4,7},{5,4},{6,5},{7,6},{8,11},{9,8},{10,9... | collective-permute-start | bytes 294920 | tf_op jit(solution)/shard_map/ppermute | solution.py:47
  117.2 3.3 %collective-permute-done.13 = f32[16,1536]{1,0:T(8,128)S(1)} collective-permute-done((f32[16,1536]{1,0:T(8,128)S(1)}, f32[16,1536]{1,0:T(8,128)S(1)}, u32[]{:S(2)}, u32[]{:S(2)}) %collective-permute-start.13) | collective-permute-done | bytes 98336 | tf_op jit(solution)/shard_map/ppermute | solution.py:47
  120.5 1.0 collective-permute-done.14
  121.5 7.2 %collective-permute-start.15 = (f32[16,1536]{1,0:T(8,128)S(1)}, f32[16,1536]{1,0:T(8,128)S(1)}, u32[]{:S(2)}, u32[]{:S(2)}) collective-permute-start(f32[16,1536]{1,0:T(8,128)S(1)} %add_add_fusion.1), channel_id=1, source_target_pairs={{0,4},{1,5},{2,6},{3,7},{4,0},{5,1},{6,2},{7,3},{8,12},{9,13},{10,... | collective-permute-start | bytes 294920 | tf_op jit(solution)/shard_map/ppermute | solution.py:47
  129.3 1.4 scatter_custom_fusion
  131.0 1.5 collective-permute-start.16
  134.3 2.6 %collective-permute-done.17 = bf16[16,1536]{1,0:T(8,128)(2,1)S(1)} collective-permute-done((bf16[16,1536]{1,0:T(8,128)(2,1)S(1)}, bf16[16,1536]{1,0:T(8,128)(2,1)S(1)}, u32[]{:S(2)}, u32[]{:S(2)}) %collective-permute-start.17) | collective-permute-done | bytes 49184 | tf_op jit(solution)/shard_map/ppermute | solution.py:47
  137.0 1.1 collective-permute-done.18
  138.3 0.9 collective-permute-start.20
  139.7 1.3 convert_reduce_fusion
  141.0 2.5 collective-permute-done.19
  143.5 1.6 collective-permute-done.20
  145.2 5.7 %collective-permute-done.21 = bf16[64,1536]{1,0:T(8,128)(2,1)S(1)} collective-permute-done((bf16[64,1536]{1,0:T(8,128)(2,1)S(1)}, bf16[64,1536]{1,0:T(8,128)(2,1)S(1)}, u32[]{:S(2)}, u32[]{:S(2)}) %collective-permute-start.21) | collective-permute-done | bytes 196640 | tf_op jit(solution)/shard_map/ppermute | solution.py:47
  152.0 4.5 %gather_fusion.2 = f32[512]{0:T(512)S(1)} fusion(f32[256,16]{0,1:T(8,128)S(1)} %fusion.93, s32[512]{0:T(512)S(1)} %reshape.371), kind=kCustom, calls=%fused_computation.2 | custom fusion | bytes 8192 | tf_op jit(solution)/shard_map/jit(take_along_axis)/gather | solution.py:260
  158.5 1.4 convolution_bitcast_fusion
  161.8 1.2 scatter_custom_fusion.1
  163.1 0.9 collective-permute-start.23
  164.8 4.4 %collective-permute-done.23 = f32[64,768]{1,0:T(8,128)S(1)} collective-permute-done((f32[64,768]{1,0:T(8,128)S(1)}, f32[64,768]{1,0:T(8,128)S(1)}, u32[]{:S(2)}, u32[]{:S(2)}) %collective-permute-start.23) | collective-permute-done | bytes 196640 | tf_op jit(solution)/shard_map/ppermute | solution.py:47
  169.3 2.1 collective-permute-done.24
  171.4 5.3 %collective-permute-done.25 = f32[64,768]{1,0:T(8,128)} collective-permute-done((f32[64,768]{1,0:T(8,128)S(1)}, f32[64,768]{1,0:T(8,128)}, u32[]{:S(2)}, u32[]{:S(2)}) %collective-permute-start.25) | collective-permute-done | bytes 196640 | tf_op jit(solution)/shard_map/ppermute | solution.py:47
  176.6 1.0 add_add_fusion
  179.5 1.2 collective-permute-done.26
  180.7 2.0 collective-permute-done.27
  185.0 0.9 collective-permute-done.29
  185.9 1.8 collective-permute-done.30
  188.5 5.5 %psum.7 = f32[4]{0:T(128)S(1)} all-reduce(f32[4]{0:T(128)S(1)} %get-tuple-element.10), channel_id=1, replica_groups=mesh['seq'=16,'row'=2,'col'=4] {'row'}, use_global_device_ids=true, to_apply=%region_14.15 | all-reduce | flops 4 | bytes 32 | tf_op jit(solution)/shard_map/psum | solution.py:144
  194.6 1.7 collective-permute-start.32
  197.1 3.2 %collective-permute-done.33 = bf16[4,768]{1,0:T(4,128)(2,1)S(1)} collective-permute-done((bf16[4,768]{1,0:T(4,128)(2,1)S(1)}, bf16[4,768]{1,0:T(4,128)(2,1)S(1)}, u32[]{:S(2)}, u32[]{:S(2)}) %collective-permute-start.33) | collective-permute-done | bytes 6176 | tf_op jit(solution)/shard_map/ppermute | solution.py:47
  200.7 1.7 collective-permute-start.35
  203.5 3.1 %collective-permute-done.36 = bf16[16,768]{1,0:T(8,128)(2,1)S(1)} collective-permute-done((bf16[16,768]{1,0:T(8,128)(2,1)S(1)}, bf16[16,768]{1,0:T(8,128)(2,1)S(1)}, u32[]{:S(2)}, u32[]{:S(2)}) %collective-permute-start.36) | collective-permute-done | bytes 24608 | tf_op jit(solution)/shard_map/ppermute | solution.py:47
  208.6 2.0 collective-permute-done.38
  210.6 1.9 collective-permute-done.39
  212.4 1.0 collective-permute-done.40
  215.0 5.2 %collective-permute-start.41 = (f32[128,1024]{1,0:T(8,128)}, f32[128,1024]{1,0:T(8,128)S(1)}, u32[]{:S(2)}, u32[]{:S(2)}) collective-permute-start(f32[128,1024]{1,0:T(8,128)} %constant_dynamic-slice_fusion), channel_id=1, source_target_pairs={{0,4},{4,0},{1,5},{5,1},{2,6},{6,2},{3,7},{7,3},{8,12},{12,8},{9,1... | collective-permute-start | bytes 1572872 | tf_op jit(solution)/shard_map/ppermute | solution.py:47
  220.3 1.7 collective-permute-done.41
  222.8 0.9 collective-permute-start.43
  224.9 1.8 collective-permute-done.43
  229.9 1.9 collective-permute-done.46
  232.4 1.3 collective-permute-start.48
  235.2 2.5 collective-permute-done.49
  238.1 6.5 %all-gather.1 = f32[1,256]{1,0:T(1,128)S(1)} all-gather(f32[1,128]{1,0:T(1,128)S(1)} %fusion.57), channel_id=3, replica_groups=mesh['seq'=16,'row'=2,'col'=4] {'row'}, dimensions={1}, use_global_device_ids=true | all-gather | bytes 1536 | tf_op jit(solution)/shard_map/all_gather | solution.py:325
  (247 shorter events, 47.7 us)
Async XLA Ops:
  7.2 206.4 %copy-start = (bf16[768,1024]{1,0:T(8,128)(2,1)S(1)}, bf16[768,1024]{1,0:T(8,128)(2,1)}, u32[]{:S(2)}) copy-start(bf16[768,1024]{1,0:T(8,128)(2,1)} %param.28) | copy-start | bytes 4718596
  7.2 52.2 %all-gather.4.cloned.1.call-start = ((), (), s32[]{:S(2)}) async-start(), calls=%async_computation | async-start | bytes 1880064 | tf_op jit(solution)/shard_map/all_gather | solution.py:192
  11.0 8.9 %collective-permute-start.6 = (bf16[1,192,96]{2,1,0:T(8,128)(2,1)}, bf16[1,192,96]{2,1,0:T(8,128)(2,1)S(1)}, u32[]{:S(2)}, u32[]{:S(2)}) collective-permute-start(bf16[1,192,96]{2,1,0:T(8,128)(2,1)} %bitcast.64), channel_id=1, source_target_pairs={{0,24},{8,0},{16,8},{24,16},{32,56},{40,32},{48,40},{56,48},{64,88... | collective-permute-start | bytes 110600 | tf_op jit(solution)/shard_map/ppermute | solution.py:47
  15.6 4.8 %collective-permute-start.7 = (bf16[1,192,96]{2,1,0:T(8,128)(2,1)}, bf16[1,192,96]{2,1,0:T(8,128)(2,1)S(1)}, u32[]{:S(2)}, u32[]{:S(2)}) collective-permute-start(bf16[1,192,96]{2,1,0:T(8,128)(2,1)} %bitcast.65), channel_id=1, source_target_pairs={{0,16},{8,24},{16,0},{24,8},{32,48},{40,56},{48,32},{56,40},{64,80... | collective-permute-start | bytes 110600 | tf_op jit(solution)/shard_map/ppermute | solution.py:47
  15.6 4.9 %collective-permute-start.8 = (bf16[1,192,96]{2,1,0:T(8,128)(2,1)}, bf16[1,192,96]{2,1,0:T(8,128)(2,1)S(1)}, u32[]{:S(2)}, u32[]{:S(2)}) collective-permute-start(bf16[1,192,96]{2,1,0:T(8,128)(2,1)} %bitcast.66), channel_id=1, source_target_pairs={{0,8},{8,16},{16,24},{24,0},{32,40},{40,48},{48,56},{56,32},{64,72... | collective-permute-start | bytes 110600 | tf_op jit(solution)/shard_map/ppermute | solution.py:47
  21.3 36.3 %copy-start.10 = (bf16[1,192,96]{2,1,0:T(8,128)(2,1)}, bf16[1,192,96]{2,1,0:T(8,128)(2,1)S(1)}, u32[]{:S(2)}) copy-start(bf16[1,192,96]{2,1,0:T(8,128)(2,1)S(1)} %get-tuple-element.58) | copy-start | bytes 110596
  21.4 36.3 %copy-start.12 = (bf16[1,192,96]{2,1,0:T(8,128)(2,1)}, bf16[1,192,96]{2,1,0:T(8,128)(2,1)S(1)}, u32[]{:S(2)}) copy-start(bf16[1,192,96]{2,1,0:T(8,128)(2,1)S(1)} %get-tuple-element.59) | copy-start | bytes 110596
  21.4 36.3 %copy-start.14 = (bf16[1,192,96]{2,1,0:T(8,128)(2,1)}, bf16[1,192,96]{2,1,0:T(8,128)(2,1)S(1)}, u32[]{:S(2)}) copy-start(bf16[1,192,96]{2,1,0:T(8,128)(2,1)S(1)} %get-tuple-element.60) | copy-start | bytes 110596
  21.4 36.3 %copy-start.16 = (bf16[1,192,96]{2,1,0:T(8,128)(2,1)}, bf16[1,192,96]{2,1,0:T(8,128)(2,1)S(1)}, u32[]{:S(2)}) copy-start(bf16[1,192,96]{2,1,0:T(8,128)(2,1)S(1)} %get-tuple-element.61) | copy-start | bytes 110596
  21.4 36.2 %collective-permute-start.9 = (bf16[4,192,96]{2,1,0:T(8,128)(2,1)S(1)}, bf16[4,192,96]{2,1,0:T(8,128)(2,1)S(1)}, u32[]{:S(2)}, u32[]{:S(2)}) collective-permute-start(bf16[4,192,96]{2,1,0:T(8,128)(2,1)S(1)} %pad_maximum_fusion.2), channel_id=1, source_target_pairs={{0,96},{8,104},{16,112},{24,120},{32,0},{40,8},{48,16},{56,24},{64... | collective-permute-start | bytes 442376 | tf_op jit(solution)/shard_map/ppermute | solution.py:47
  24.3 33.4 %collective-permute-start.10 = (bf16[4,192,96]{2,1,0:T(8,128)(2,1)S(1)}, bf16[4,192,96]{2,1,0:T(8,128)(2,1)S(1)}, u32[]{:S(2)}, u32[]{:S(2)}) collective-permute-start(bf16[4,192,96]{2,1,0:T(8,128)(2,1)S(1)} %pad_maximum_fusion.2), channel_id=1, source_target_pairs={{0,64},{8,72},{16,80},{24,88},{32,96},{40,104},{48,112},{56,120},{... | collective-permute-start | bytes 442376 | tf_op jit(solution)/shard_map/ppermute | solution.py:47
  24.6 33.1 %collective-permute-start.11 = (bf16[4,192,96]{2,1,0:T(8,128)(2,1)S(1)}, bf16[4,192,96]{2,1,0:T(8,128)(2,1)S(1)}, u32[]{:S(2)}, u32[]{:S(2)}) collective-permute-start(bf16[4,192,96]{2,1,0:T(8,128)(2,1)S(1)} %pad_maximum_fusion.2), channel_id=1, source_target_pairs={{0,32},{8,40},{16,48},{24,56},{32,64},{40,72},{48,80},{56,88},{64,... | collective-permute-start | bytes 442376 | tf_op jit(solution)/shard_map/ppermute | solution.py:47
  90.4 17.5 %copy-start.2 = (bf16[4,192,96]{2,1,0:T(8,128)(2,1)S(1)}, bf16[4,192,96]{2,1,0:T(8,128)(2,1)}, u32[]{:S(2)}) copy-start(bf16[4,192,96]{2,1,0:T(8,128)(2,1)} %get-tuple-element.36) | copy-start | bytes 442372
  90.4 17.5 %copy-start.3 = (bf16[4,192,96]{2,1,0:T(8,128)(2,1)S(1)}, bf16[4,192,96]{2,1,0:T(8,128)(2,1)}, u32[]{:S(2)}) copy-start(bf16[4,192,96]{2,1,0:T(8,128)(2,1)} %get-tuple-element.37) | copy-start | bytes 442372
  94.6 36.1 %copy-start.18 = (bf16[16,1536]{1,0:T(8,128)(2,1)S(1)}, bf16[16,1536]{1,0:T(8,128)(2,1)}, u32[]{:S(2)}) copy-start(bf16[16,1536]{1,0:T(8,128)(2,1)} %param.15) | copy-start | bytes 147460
  95.7 3.9 %collective-permute-start = (f32[16,792]{1,0:T(8,128)S(1)}, f32[16,792]{1,0:T(8,128)S(1)}, u32[]{:S(2)}, u32[]{:S(2)}) collective-permute-start(f32[16,792]{1,0:T(8,128)S(1)} %get-tuple-element.50), channel_id=1, source_target_pairs={{0,96},{8,104},{16,112},{24,120},{32,0},{40,8},{48,16},{56,24},{64... | collective-permute-start | bytes 152072 | tf_op jit(solution)/shard_map/ppermute | solution.py:47
  98.3 4.6 %collective-permute-start.1 = (f32[16,792]{1,0:T(8,128)S(1)}, f32[16,792]{1,0:T(8,128)S(1)}, u32[]{:S(2)}, u32[]{:S(2)}) collective-permute-start(f32[16,792]{1,0:T(8,128)S(1)} %get-tuple-element.49), channel_id=1, source_target_pairs={{0,64},{8,72},{16,80},{24,88},{32,96},{40,104},{48,112},{56,120},{... | collective-permute-start | bytes 152072 | tf_op jit(solution)/shard_map/ppermute | solution.py:47
  98.9 4.6 %collective-permute-start.2 = (f32[16,792]{1,0:T(8,128)S(1)}, f32[16,792]{1,0:T(8,128)S(1)}, u32[]{:S(2)}, u32[]{:S(2)}) collective-permute-start(f32[16,792]{1,0:T(8,128)S(1)} %get-tuple-element.48), channel_id=1, source_target_pairs={{0,32},{8,40},{16,48},{24,56},{32,64},{40,72},{48,80},{56,88},{64,... | collective-permute-start | bytes 152072 | tf_op jit(solution)/shard_map/ppermute | solution.py:47
  99.2 31.7 %copy-start.21 = (f32[1536]{0:T(1024)S(1)}, f32[1536]{0:T(1024)}, u32[]{:S(2)}) copy-start(f32[1536]{0:T(1024)} %param.22) | copy-start | bytes 18436
  105.0 46.3 %copy-start.20 = (f32[1536,16]{0,1:T(8,128)S(1)}, f32[1536,16]{0,1:T(8,128)}, u32[]{:S(2)}) copy-start(f32[1536,16]{0,1:T(8,128)} %param.23) | copy-start | bytes 294916
  105.0 4.5 %collective-permute-start.3 = (f32[4,792]{1,0:T(4,128)S(1)}, f32[4,792]{1,0:T(4,128)S(1)}, u32[]{:S(2)}, u32[]{:S(2)}) collective-permute-start(f32[4,792]{1,0:T(4,128)S(1)} %get-tuple-element.74), channel_id=1, source_target_pairs={{0,24},{8,0},{16,8},{24,16},{32,56},{40,32},{48,40},{56,48},{64,88... | collective-permute-start | bytes 38024 | tf_op jit(solution)/shard_map/ppermute | solution.py:47
  106.2 4.1 %collective-permute-start.4 = (f32[4,792]{1,0:T(4,128)S(1)}, f32[4,792]{1,0:T(4,128)S(1)}, u32[]{:S(2)}, u32[]{:S(2)}) collective-permute-start(f32[4,792]{1,0:T(4,128)S(1)} %get-tuple-element.73), channel_id=1, source_target_pairs={{0,16},{8,24},{16,0},{24,8},{32,48},{40,56},{48,32},{56,40},{64,80... | collective-permute-start | bytes 38024 | tf_op jit(solution)/shard_map/ppermute | solution.py:47
  107.9 3.8 %collective-permute-start.5 = (f32[4,792]{1,0:T(4,128)S(1)}, f32[4,792]{1,0:T(4,128)S(1)}, u32[]{:S(2)}, u32[]{:S(2)}) collective-permute-start(f32[4,792]{1,0:T(4,128)S(1)} %get-tuple-element.72), channel_id=1, source_target_pairs={{0,8},{8,16},{16,24},{24,0},{32,40},{40,48},{48,56},{56,32},{64,72... | collective-permute-start | bytes 38024 | tf_op jit(solution)/shard_map/ppermute | solution.py:47
  112.8 4.4 %collective-permute-start.12 = (f32[16,1536]{1,0:T(8,128)S(1)}, f32[16,1536]{1,0:T(8,128)S(1)}, u32[]{:S(2)}, u32[]{:S(2)}) collective-permute-start(f32[16,1536]{1,0:T(8,128)S(1)} %fusion.92), channel_id=1, source_target_pairs={{0,3},{1,0},{2,1},{3,2},{4,7},{5,4},{6,5},{7,6},{8,11},{9,8},{10,9... | collective-permute-start | bytes 294920 | tf_op jit(solution)/shard_map/ppermute | solution.py:47
  115.4 5.1 %collective-permute-start.13 = (f32[16,1536]{1,0:T(8,128)S(1)}, f32[16,1536]{1,0:T(8,128)S(1)}, u32[]{:S(2)}, u32[]{:S(2)}) collective-permute-start(f32[16,1536]{1,0:T(8,128)S(1)} %fusion.92), channel_id=1, source_target_pairs={{0,2},{1,3},{2,0},{3,1},{4,6},{5,7},{6,4},{7,5},{8,10},{9,11},{10,... | collective-permute-start | bytes 294920 | tf_op jit(solution)/shard_map/ppermute | solution.py:47
  115.9 5.6 %collective-permute-start.14 = (f32[16,1536]{1,0:T(8,128)S(1)}, f32[16,1536]{1,0:T(8,128)S(1)}, u32[]{:S(2)}, u32[]{:S(2)}) collective-permute-start(f32[16,1536]{1,0:T(8,128)S(1)} %fusion.92), channel_id=1, source_target_pairs={{0,1},{1,2},{2,3},{3,0},{4,5},{5,6},{6,7},{7,4},{8,9},{9,10},{10,1... | collective-permute-start | bytes 294920 | tf_op jit(solution)/shard_map/ppermute | solution.py:47
  121.5 9.2 %collective-permute-start.15 = (f32[16,1536]{1,0:T(8,128)S(1)}, f32[16,1536]{1,0:T(8,128)S(1)}, u32[]{:S(2)}, u32[]{:S(2)}) collective-permute-start(f32[16,1536]{1,0:T(8,128)S(1)} %add_add_fusion.1), channel_id=1, source_target_pairs={{0,4},{1,5},{2,6},{3,7},{4,0},{5,1},{6,2},{7,3},{8,12},{9,13},{10,... | collective-permute-start | bytes 294920 | tf_op jit(solution)/shard_map/ppermute | solution.py:47
  131.0 3.4 %collective-permute-start.16 = (bf16[16,1536]{1,0:T(8,128)(2,1)S(1)}, bf16[16,1536]{1,0:T(8,128)(2,1)S(1)}, u32[]{:S(2)}, u32[]{:S(2)}) collective-permute-start(bf16[16,1536]{1,0:T(8,128)(2,1)S(1)} %multiply_convert_fusion), channel_id=1, source_target_pairs={{0,24},{8,0},{16,8},{24,16},{32,56},{40,32},{48,40},{56,48},{64,88... | collective-permute-start | bytes 147464 | tf_op jit(solution)/shard_map/ppermute | solution.py:47
  132.5 4.5 %collective-permute-start.17 = (bf16[16,1536]{1,0:T(8,128)(2,1)S(1)}, bf16[16,1536]{1,0:T(8,128)(2,1)S(1)}, u32[]{:S(2)}, u32[]{:S(2)}) collective-permute-start(bf16[16,1536]{1,0:T(8,128)(2,1)S(1)} %multiply_convert_fusion), channel_id=1, source_target_pairs={{0,16},{8,24},{16,0},{24,8},{32,48},{40,56},{48,32},{56,40},{64,80... | collective-permute-start | bytes 147464 | tf_op jit(solution)/shard_map/ppermute | solution.py:47
  133.1 4.9 %collective-permute-start.18 = (bf16[16,1536]{1,0:T(8,128)(2,1)S(1)}, bf16[16,1536]{1,0:T(8,128)(2,1)S(1)}, u32[]{:S(2)}, u32[]{:S(2)}) collective-permute-start(bf16[16,1536]{1,0:T(8,128)(2,1)S(1)} %multiply_convert_fusion), channel_id=1, source_target_pairs={{0,8},{8,16},{16,24},{24,0},{32,40},{40,48},{48,56},{56,32},{64,72... | collective-permute-start | bytes 147464 | tf_op jit(solution)/shard_map/ppermute | solution.py:47
  138.2 5.4 %collective-permute-start.19 = (bf16[64,1536]{1,0:T(8,128)(2,1)S(1)}, bf16[64,1536]{1,0:T(8,128)(2,1)S(1)}, u32[]{:S(2)}, u32[]{:S(2)}) collective-permute-start(bf16[64,1536]{1,0:T(8,128)(2,1)S(1)} %pad_maximum_fusion.3), channel_id=1, source_target_pairs={{0,96},{8,104},{16,112},{24,120},{32,0},{40,8},{48,16},{56,24},{64... | collective-permute-start | bytes 589832 | tf_op jit(solution)/shard_map/ppermute | solution.py:47
  138.3 6.9 %collective-permute-start.20 = (bf16[64,1536]{1,0:T(8,128)(2,1)S(1)}, bf16[64,1536]{1,0:T(8,128)(2,1)S(1)}, u32[]{:S(2)}, u32[]{:S(2)}) collective-permute-start(bf16[64,1536]{1,0:T(8,128)(2,1)S(1)} %pad_maximum_fusion.3), channel_id=1, source_target_pairs={{0,64},{8,72},{16,80},{24,88},{32,96},{40,104},{48,112},{56,120},{... | collective-permute-start | bytes 589832 | tf_op jit(solution)/shard_map/ppermute | solution.py:47
  139.2 11.7 %collective-permute-start.21 = (bf16[64,1536]{1,0:T(8,128)(2,1)S(1)}, bf16[64,1536]{1,0:T(8,128)(2,1)S(1)}, u32[]{:S(2)}, u32[]{:S(2)}) collective-permute-start(bf16[64,1536]{1,0:T(8,128)(2,1)S(1)} %pad_maximum_fusion.3), channel_id=1, source_target_pairs={{0,32},{8,40},{16,48},{24,56},{32,64},{40,72},{48,80},{56,88},{64,... | collective-permute-start | bytes 589832 | tf_op jit(solution)/shard_map/ppermute | solution.py:47
  156.6 28.3 %copy-start.25 = (f32[1536]{0:T(1024)S(1)}, f32[1536]{0:T(1024)}, u32[]{:S(2)}) copy-start(f32[1536]{0:T(1024)} %param.27) | copy-start | bytes 18436
  158.5 61.8 %copy-start.27 = (s32[256]{0:T(256)S(1)}, s32[256]{0:T(256)}, u32[]{:S(2)}) copy-start(s32[256]{0:T(256)} %param.29) | copy-start | bytes 3076
  159.9 1.7 collective-permute-start.22
  163.1 6.2 %collective-permute-start.23 = (f32[64,768]{1,0:T(8,128)S(1)}, f32[64,768]{1,0:T(8,128)S(1)}, u32[]{:S(2)}, u32[]{:S(2)}) collective-permute-start(f32[64,768]{1,0:T(8,128)S(1)} %get-tuple-element.31), channel_id=1, source_target_pairs={{0,96},{1,97},{2,98},{3,99},{8,104},{9,105},{10,106},{11,107},{16,... | collective-permute-start | bytes 589832 | tf_op jit(solution)/shard_map/ppermute | solution.py:47
  164.0 7.4 %collective-permute-start.24 = (f32[64,768]{1,0:T(8,128)S(1)}, f32[64,768]{1,0:T(8,128)S(1)}, u32[]{:S(2)}, u32[]{:S(2)}) collective-permute-start(f32[64,768]{1,0:T(8,128)S(1)} %get-tuple-element.30), channel_id=1, source_target_pairs={{0,64},{1,65},{2,66},{3,67},{8,72},{9,73},{10,74},{11,75},{16,80},... | collective-permute-start | bytes 589832 | tf_op jit(solution)/shard_map/ppermute | solution.py:47
  164.3 12.3 %collective-permute-start.25 = (f32[64,768]{1,0:T(8,128)S(1)}, f32[64,768]{1,0:T(8,128)}, u32[]{:S(2)}, u32[]{:S(2)}) collective-permute-start(f32[64,768]{1,0:T(8,128)S(1)} %get-tuple-element.29), channel_id=1, source_target_pairs={{0,32},{1,33},{2,34},{3,35},{8,40},{9,41},{10,42},{11,43},{16,48},... | collective-permute-start | bytes 589832 | tf_op jit(solution)/shard_map/ppermute | solution.py:47
  177.7 3.0 %collective-permute-start.26 = (f32[16,768]{1,0:T(8,128)S(1)}, f32[16,768]{1,0:T(8,128)S(1)}, u32[]{:S(2)}, u32[]{:S(2)}) collective-permute-start(f32[16,768]{1,0:T(8,128)S(1)} %get-tuple-element.53), channel_id=1, source_target_pairs={{0,24},{1,25},{2,26},{3,27},{8,0},{9,1},{10,2},{11,3},{16,8},{17,9... | collective-permute-start | bytes 147464 | tf_op jit(solution)/shard_map/ppermute | solution.py:47
  178.2 4.5 %collective-permute-start.27 = (f32[16,768]{1,0:T(8,128)S(1)}, f32[16,768]{1,0:T(8,128)S(1)}, u32[]{:S(2)}, u32[]{:S(2)}) collective-permute-start(f32[16,768]{1,0:T(8,128)S(1)} %get-tuple-element.52), channel_id=1, source_target_pairs={{0,16},{1,17},{2,18},{3,19},{8,24},{9,25},{10,26},{11,27},{16,0},{... | collective-permute-start | bytes 147464 | tf_op jit(solution)/shard_map/ppermute | solution.py:47
  178.7 4.5 %collective-permute-start.28 = (f32[16,768]{1,0:T(8,128)S(1)}, f32[16,768]{1,0:T(8,128)S(1)}, u32[]{:S(2)}, u32[]{:S(2)}) collective-permute-start(f32[16,768]{1,0:T(8,128)S(1)} %get-tuple-element.51), channel_id=1, source_target_pairs={{0,8},{1,9},{2,10},{3,11},{8,16},{9,17},{10,18},{11,19},{16,24},{1... | collective-permute-start | bytes 147464 | tf_op jit(solution)/shard_map/ppermute | solution.py:47
  183.3 2.6 %collective-permute-start.29 = (f32[4,768]{1,0:T(4,128)S(1)}, f32[4,768]{1,0:T(4,128)S(1)}, u32[]{:S(2)}, u32[]{:S(2)}) collective-permute-start(f32[4,768]{1,0:T(4,128)S(1)} %get-tuple-element.77), channel_id=1, source_target_pairs={{0,3},{1,0},{2,1},{3,2},{8,11},{9,8},{10,9},{11,10},{16,19},{17,16... | collective-permute-start | bytes 36872 | tf_op jit(solution)/shard_map/ppermute | solution.py:47
  183.6 4.0 %collective-permute-start.30 = (f32[4,768]{1,0:T(4,128)S(1)}, f32[4,768]{1,0:T(4,128)S(1)}, u32[]{:S(2)}, u32[]{:S(2)}) collective-permute-start(f32[4,768]{1,0:T(4,128)S(1)} %get-tuple-element.76), channel_id=1, source_target_pairs={{0,2},{1,3},{2,0},{3,1},{8,10},{9,11},{10,8},{11,9},{16,18},{17,19... | collective-permute-start | bytes 36872 | tf_op jit(solution)/shard_map/ppermute | solution.py:47
  184.2 4.1 %collective-permute-start.31 = (f32[4,768]{1,0:T(4,128)S(1)}, f32[4,768]{1,0:T(4,128)S(1)}, u32[]{:S(2)}, u32[]{:S(2)}) collective-permute-start(f32[4,768]{1,0:T(4,128)S(1)} %get-tuple-element.75), channel_id=1, source_target_pairs={{0,1},{1,2},{2,3},{3,0},{8,9},{9,10},{10,11},{11,8},{16,17},{17,18... | collective-permute-start | bytes 36872 | tf_op jit(solution)/shard_map/ppermute | solution.py:47
  194.6 2.5 collective-permute-start.32
  196.3 4.0 %collective-permute-start.33 = (bf16[4,768]{1,0:T(4,128)(2,1)S(1)}, bf16[4,768]{1,0:T(4,128)(2,1)S(1)}, u32[]{:S(2)}, u32[]{:S(2)}) collective-permute-start(bf16[4,768]{1,0:T(4,128)(2,1)S(1)} %get-tuple-element.82), channel_id=1, source_target_pairs={{0,2},{1,3},{2,0},{3,1},{8,10},{9,11},{10,8},{11,9},{16,18},{17,19... | collective-permute-start | bytes 18440 | tf_op jit(solution)/shard_map/ppermute | solution.py:47
  197.0 3.7 %collective-permute-start.34 = (bf16[4,768]{1,0:T(4,128)(2,1)S(1)}, bf16[4,768]{1,0:T(4,128)(2,1)S(1)}, u32[]{:S(2)}, u32[]{:S(2)}) collective-permute-start(bf16[4,768]{1,0:T(4,128)(2,1)S(1)} %get-tuple-element.82), channel_id=1, source_target_pairs={{0,1},{1,2},{2,3},{3,0},{8,9},{9,10},{10,11},{11,8},{16,17},{17,18... | collective-permute-start | bytes 18440 | tf_op jit(solution)/shard_map/ppermute | solution.py:47
  200.7 2.7 %collective-permute-start.35 = (bf16[16,768]{1,0:T(8,128)(2,1)S(1)}, bf16[16,768]{1,0:T(8,128)(2,1)S(1)}, u32[]{:S(2)}, u32[]{:S(2)}) collective-permute-start(bf16[16,768]{1,0:T(8,128)(2,1)S(1)} %pad_maximum_fusion.8), channel_id=1, source_target_pairs={{0,24},{1,25},{2,26},{3,27},{8,0},{9,1},{10,2},{11,3},{16,8},{17,9... | collective-permute-start | bytes 73736 | tf_op jit(solution)/shard_map/ppermute | solution.py:47
  202.4 4.2 %collective-permute-start.36 = (bf16[16,768]{1,0:T(8,128)(2,1)S(1)}, bf16[16,768]{1,0:T(8,128)(2,1)S(1)}, u32[]{:S(2)}, u32[]{:S(2)}) collective-permute-start(bf16[16,768]{1,0:T(8,128)(2,1)S(1)} %pad_maximum_fusion.8), channel_id=1, source_target_pairs={{0,16},{1,17},{2,18},{3,19},{8,24},{9,25},{10,26},{11,27},{16,0},{... | collective-permute-start | bytes 73736 | tf_op jit(solution)/shard_map/ppermute | solution.py:47
  203.0 3.9 %collective-permute-start.37 = (bf16[16,768]{1,0:T(8,128)(2,1)S(1)}, bf16[16,768]{1,0:T(8,128)(2,1)S(1)}, u32[]{:S(2)}, u32[]{:S(2)}) collective-permute-start(bf16[16,768]{1,0:T(8,128)(2,1)S(1)} %pad_maximum_fusion.8), channel_id=1, source_target_pairs={{0,8},{1,9},{2,10},{3,11},{8,16},{9,17},{10,18},{11,19},{16,24},{1... | collective-permute-start | bytes 73736 | tf_op jit(solution)/shard_map/ppermute | solution.py:47
  207.0 3.5 %collective-permute-start.38 = (bf16[64,768]{1,0:T(8,128)(2,1)S(1)}, bf16[64,768]{1,0:T(8,128)(2,1)S(1)}, u32[]{:S(2)}, u32[]{:S(2)}) collective-permute-start(bf16[64,768]{1,0:T(8,128)(2,1)S(1)} %pad_maximum_fusion.5), channel_id=1, source_target_pairs={{0,96},{1,97},{2,98},{3,99},{8,104},{9,105},{10,106},{11,107},{16,... | collective-permute-start | bytes 294920 | tf_op jit(solution)/shard_map/ppermute | solution.py:47
  207.4 5.0 %collective-permute-start.39 = (bf16[64,768]{1,0:T(8,128)(2,1)S(1)}, bf16[64,768]{1,0:T(8,128)(2,1)S(1)}, u32[]{:S(2)}, u32[]{:S(2)}) collective-permute-start(bf16[64,768]{1,0:T(8,128)(2,1)S(1)} %pad_maximum_fusion.5), channel_id=1, source_target_pairs={{0,64},{1,65},{2,66},{3,67},{8,72},{9,73},{10,74},{11,75},{16,80},... | collective-permute-start | bytes 294920 | tf_op jit(solution)/shard_map/ppermute | solution.py:47
  207.7 5.7 %collective-permute-start.40 = (bf16[64,768]{1,0:T(8,128)(2,1)S(1)}, bf16[64,768]{1,0:T(8,128)(2,1)S(1)}, u32[]{:S(2)}, u32[]{:S(2)}) collective-permute-start(bf16[64,768]{1,0:T(8,128)(2,1)S(1)} %pad_maximum_fusion.5), channel_id=1, source_target_pairs={{0,32},{1,33},{2,34},{3,35},{8,40},{9,41},{10,42},{11,43},{16,48},... | collective-permute-start | bytes 294920 | tf_op jit(solution)/shard_map/ppermute | solution.py:47
  215.0 6.9 %collective-permute-start.41 = (f32[128,1024]{1,0:T(8,128)}, f32[128,1024]{1,0:T(8,128)S(1)}, u32[]{:S(2)}, u32[]{:S(2)}) collective-permute-start(f32[128,1024]{1,0:T(8,128)} %constant_dynamic-slice_fusion), channel_id=1, source_target_pairs={{0,4},{4,0},{1,5},{5,1},{2,6},{6,2},{3,7},{7,3},{8,12},{12,8},{9,1... | collective-permute-start | bytes 1572872 | tf_op jit(solution)/shard_map/ppermute | solution.py:47
  222.4 2.5 collective-permute-start.42
  222.8 3.9 %collective-permute-start.43 = (f32[1,384]{1,0:T(1,128)S(1)}, f32[1,384]{1,0:T(1,128)S(1)}, u32[]{:S(2)}, u32[]{:S(2)}) collective-permute-start(f32[1,384]{1,0:T(1,128)S(1)} %pad_maximum_fusion.9), channel_id=1, source_target_pairs={{0,2},{1,3},{2,0},{3,1},{8,10},{9,11},{10,8},{11,9},{16,18},{17,19... | collective-permute-start | bytes 4616 | tf_op jit(solution)/shard_map/ppermute | solution.py:47
  223.7 3.6 %collective-permute-start.44 = (f32[1,384]{1,0:T(1,128)S(1)}, f32[1,384]{1,0:T(1,128)S(1)}, u32[]{:S(2)}, u32[]{:S(2)}) collective-permute-start(f32[1,384]{1,0:T(1,128)S(1)} %pad_maximum_fusion.9), channel_id=1, source_target_pairs={{0,1},{1,2},{2,3},{3,0},{8,9},{9,10},{10,11},{11,8},{16,17},{17,18... | collective-permute-start | bytes 4616 | tf_op jit(solution)/shard_map/ppermute | solution.py:47
  227.4 2.5 collective-permute-start.45
  227.9 3.9 %collective-permute-start.46 = (f32[1,384]{1,0:T(1,128)S(1)}, f32[1,384]{1,0:T(1,128)S(1)}, u32[]{:S(2)}, u32[]{:S(2)}) collective-permute-start(f32[1,384]{1,0:T(1,128)S(1)} %pad_maximum_fusion.10), channel_id=1, source_target_pairs={{0,16},{1,17},{2,18},{3,19},{8,24},{9,25},{10,26},{11,27},{16,0},{... | collective-permute-start | bytes 4616 | tf_op jit(solution)/shard_map/ppermute | solution.py:47
  228.7 3.6 %collective-permute-start.47 = (f32[1,384]{1,0:T(1,128)S(1)}, f32[1,384]{1,0:T(1,128)S(1)}, u32[]{:S(2)}, u32[]{:S(2)}) collective-permute-start(f32[1,384]{1,0:T(1,128)S(1)} %pad_maximum_fusion.10), channel_id=1, source_target_pairs={{0,8},{1,9},{2,10},{3,11},{8,16},{9,17},{10,18},{11,19},{16,24},{1... | collective-permute-start | bytes 4616 | tf_op jit(solution)/shard_map/ppermute | solution.py:47
  232.4 2.8 %collective-permute-start.48 = (f32[1,384]{1,0:T(1,128)S(1)}, f32[1,384]{1,0:T(1,128)S(1)}, u32[]{:S(2)}, u32[]{:S(2)}) collective-permute-start(f32[1,384]{1,0:T(1,128)S(1)} %pad_maximum_fusion.11), channel_id=1, source_target_pairs={{0,96},{1,97},{2,98},{3,99},{8,104},{9,105},{10,106},{11,107},{16,... | collective-permute-start | bytes 4616 | tf_op jit(solution)/shard_map/ppermute | solution.py:47
  233.8 3.9 %collective-permute-start.49 = (f32[1,384]{1,0:T(1,128)S(1)}, f32[1,384]{1,0:T(1,128)S(1)}, u32[]{:S(2)}, u32[]{:S(2)}) collective-permute-start(f32[1,384]{1,0:T(1,128)S(1)} %pad_maximum_fusion.11), channel_id=1, source_target_pairs={{0,64},{1,65},{2,66},{3,67},{8,72},{9,73},{10,74},{11,75},{16,80},... | collective-permute-start | bytes 4616 | tf_op jit(solution)/shard_map/ppermute | solution.py:47
  234.4 3.6 %collective-permute-start.50 = (f32[1,384]{1,0:T(1,128)S(1)}, f32[1,384]{1,0:T(1,128)S(1)}, u32[]{:S(2)}, u32[]{:S(2)}) collective-permute-start(f32[1,384]{1,0:T(1,128)S(1)} %pad_maximum_fusion.11), channel_id=1, source_target_pairs={{0,32},{1,33},{2,34},{3,35},{8,40},{9,41},{10,42},{11,43},{16,48},... | collective-permute-start | bytes 4616 | tf_op jit(solution)/shard_map/ppermute | solution.py:47
  (16 other events, 103.8 us)
Sparse Core Ops, SparseCore 0:
  11.1 48.2 all-gather.3
